TPU v7x, 512 devices: a whole 4x4x16 slice. The times are simulated.
512 devices in a mesh: space: 16 (over z), chaos: 32 (over x, y, core).
Axes of the slice: x: 4, y: 4, z: 16, core: 2. Of those that a mesh axis runs over, the one named last changes fastest.
Arguments:
- forcing: float32 [960, 64, 128], P('chaos', 'space'), may hold values from -120 to 120
- mean_field: float32 [64, 128], P('space'), may hold values from 1 to 8
- modes: float32 [12, 64, 128], P(None, 'space'), may hold values from 0.02 to 0.05
- lengths: int32 [32], replicated, may hold values from 1 to 30, 455 in all
Outputs:
- solution: float32 [960, 64, 128], P('chaos', 'space')
- norms: float32 [3], replicated
Inputs may be any that keep to these rules, and one draw needn't show every extreme that they name: Group lengths are positive, sum to 455, and the largest is exactly 30.
All inputs are finite; a program needn't handle non-finite values.
Results may differ from a plain program's by a relative error of at most 0.0001.
Values sent between devices are 32-bit elements; how exact they have to be, the bound alone decides.
No kernel may reach another device: no remote copies, remote signals or barrier semaphores. Data moves between devices by JAX's collectives and lax.ppermute only.
A program may use at most 64 MiB of HBM per device.

v0:
```python
import functools
import math

import jax
import jax.numpy as jnp
import numpy as np
from jax import lax
from jax.experimental import pallas as pl
from jax.experimental.pallas import tpu as pltpu
from jax.sharding import PartitionSpec as P

M = 12
P_SIZE = 455
ITERS = 3
GHOST = ITERS + 1


spectrum_low = 0.05
spectrum_high = 3.0


def index_key(entry):
    return tuple((int(value) for value in entry))


def chaos_tables(terms):
    indices = [np.zeros(terms, dtype=np.int64)]
    for first in range(terms):
        entry = np.zeros(terms, dtype=np.int64)
        entry[first] += 1
        indices.append(entry)
    for first in range(terms):
        for second in range(first, terms):
            entry = np.zeros(terms, dtype=np.int64)
            entry[first] += 1
            entry[second] += 1
            indices.append(entry)
    for first in range(terms):
        for second in range(first, terms):
            for third in range(second, terms):
                entry = np.zeros(terms, dtype=np.int64)
                entry[first] += 1
                entry[second] += 1
                entry[third] += 1
                indices.append(entry)
    lookup = {}
    for number, entry in enumerate(indices):
        lookup[index_key(entry)] = number
    count = len(indices)
    upward = np.full((count, terms), count, dtype=np.int64)
    downward = np.full((count, terms), count, dtype=np.int64)
    up_coef = np.zeros((count, terms))
    down_coef = np.zeros((count, terms))
    for number, entry in enumerate(indices):
        for term in range(terms):
            if entry.sum() < 3:
                other = entry.copy()
                other[term] += 1
                upward[number, term] = lookup[index_key(other)]
                up_coef[number, term] = math.sqrt(entry[term] + 1)
            if entry[term] > 0:
                other = entry.copy()
                other[term] -= 1
                downward[number, term] = lookup[index_key(other)]
                down_coef[number, term] = math.sqrt(entry[term])
    return (
        upward.astype(np.int32),
        downward.astype(np.int32),
        up_coef.astype(np.float32),
        down_coef.astype(np.float32),
    )


def degree_layout(terms):
    sizes = [1, terms, terms * (terms + 1) // 2, terms * (terms + 1) * (terms + 2) // 6]
    firsts = np.cumsum([0] + sizes[:-1])
    padded = [-(-size // 8) * 8 for size in sizes]
    offsets = np.cumsum([0] + padded[:-1])
    return sizes, firsts, padded, offsets


def coupling_blocks(terms):
    upward, downward, up_coef, down_coef = chaos_tables(terms)
    sizes, firsts, padded, offsets = degree_layout(terms)
    count = sum(sizes)
    total = sum(padded)
    row_of = np.zeros(count, np.int64)
    for d in range(4):
        row_of[firsts[d] : firsts[d] + sizes[d]] = offsets[d] + np.arange(sizes[d])
    dense = np.zeros((terms, total, total), np.float64)
    for p in range(count):
        for k in range(terms):
            if upward[p, k] < count:
                dense[k, row_of[p], row_of[upward[p, k]]] = up_coef[p, k]
            if downward[p, k] < count:
                dense[k, row_of[p], row_of[downward[p, k]]] = down_coef[p, k]

    def block(out_degrees, in_degree):
        rows = np.concatenate([offsets[d] + np.arange(padded[d]) for d in out_degrees])
        cols = offsets[in_degree] + np.arange(padded[in_degree])
        part = dense[:, rows][:, :, cols]
        return np.transpose(part, (1, 0, 2)).reshape(len(rows), terms * len(cols)).astype(np.float32)

    return {
        0: block((1,), 0),
        1: block((0, 2), 1),
        2: block((1, 3), 2),
        3: block((2,), 3),
    }, row_of, total


def neighbour(values, step):
    blank = jnp.zeros(values.shape[:-1] + (abs(step),), values.dtype)
    if step > 0:
        return jnp.concatenate([values[..., step:], blank], axis=-1)
    return jnp.concatenate([blank, values[..., :step]], axis=-1)


def sweeps(rhs_ref, field_ref, mask_ref, w0_ref, w1_ref, w2_ref, w3_ref, sol_ref, part_ref,
           s0_ref, s1_ref, s2_ref, s3_ref, *, padded, offsets, cols):
    lanes = rhs_ref.shape[1]
    shifts = (cols, lanes - cols, lanes - 1, 1)

    def near(values, shift):
        return pltpu.roll(values, shift, 1)

    fields = field_ref[...]
    inside = mask_ref[0:1, :] > 0.5
    own = mask_ref[1:2, :] > 0.5
    weights = [[0.5 * (fields[k : k + 1] + near(fields, s)[k : k + 1]) for s in shifts] for k in range(M + 1)]
    mean_now = fields[0:1]
    diagonal = 0.5 * (mean_now + near(mean_now, shifts[0]))
    for s in shifts[1:]:
        diagonal = diagonal + 0.5 * (mean_now + near(mean_now, s))
    diagonal = jnp.where(inside, diagonal, 1.0)
    stacks = (s0_ref, s1_ref, s2_ref, s3_ref)
    mats = (w0_ref, w1_ref, w2_ref, w3_ref)

    def operator(tiles):
        diffs = [tiles - near(tiles, s) for s in shifts]
        base = None
        for k in range(M + 1):
            term = weights[k][0] * diffs[0]
            for n in range(1, 4):
                term = term + weights[k][n] * diffs[n]
            if k == 0:
                base = term
                continue
            for d in range(4):
                stacks[d][(k - 1) * padded[d] : k * padded[d], :] = term[offsets[d] : offsets[d] + padded[d]]
        mixed = [
            jnp.dot(mats[d][...], stacks[d][...], precision=lax.Precision.HIGHEST, preferred_element_type=jnp.float32)
            for d in range(4)
        ]
        p0, p1 = padded[0], padded[1]
        coupled = jnp.concatenate(
            [mixed[1][:p0], mixed[2][:p1] + mixed[0], mixed[3] + mixed[1][p0:], mixed[2][p1:]], axis=0
        )
        return base + coupled

    theta = (spectrum_high + spectrum_low) / 2.0
    delta = (spectrum_high - spectrum_low) / 2.0
    sigma = theta / delta
    rho = 1.0 / sigma
    residual = rhs_ref[...]
    solution = jnp.zeros_like(residual)
    direction = jnp.where(inside, residual / diagonal / theta, 0.0)
    lane = lax.broadcasted_iota(jnp.int32, (8, 128), 1)
    partial_out = jnp.zeros((8, 128), jnp.float32)
    for sweep_index in range(ITERS):
        solution = solution + direction
        residual = residual - operator(direction)
        value = jnp.sum(jnp.where(own, residual * residual, 0.0))
        partial_out = jnp.where(lane == sweep_index, value, partial_out)
        if sweep_index + 1 < ITERS:
            rho_new = 1.0 / (2.0 * sigma - rho)
            direction = rho_new * rho * direction + 2.0 * rho_new / delta * (residual / diagonal)
            direction = jnp.where(inside, direction, 0.0)
            rho = rho_new
    sol_ref[...] = solution
    part_ref[...] = partial_out


def local(forcing, mean_field, modes, lengths):
    cap, rows, cols = forcing.shape
    n_space = lax.axis_size("space")
    n_chaos = lax.axis_size("chaos")
    my_row_block = lax.axis_index("space")
    my_col_block = lax.axis_index("chaos")
    width = cols // n_chaos
    ghost = GHOST
    assert rows >= ghost and ghost % width == 0 and width * n_chaos == cols
    patch_rows, patch_cols = rows + 2 * ghost, width + 2 * ghost
    cells = patch_rows * patch_cols
    count = P_SIZE

    fields = jnp.concatenate([mean_field[None], mean_field[None] * modes], axis=0)
    block = jnp.concatenate([forcing, fields], axis=0)
    down_pairs = [(i, i + 1) for i in range(n_space - 1)]
    up_pairs = [(i + 1, i) for i in range(n_space - 1)]
    above = lax.ppermute(block[:, rows - ghost :], "space", down_pairs)
    below = lax.ppermute(block[:, :ghost], "space", up_pairs)
    tall = jnp.concatenate([above, block, below], axis=1)
    tall = jnp.pad(tall, ((0, 0), (0, 0), (ghost, ghost)))

    side = ghost // width
    pieces = tall.reshape(tall.shape[0], patch_rows, n_chaos + 2 * side, width)
    windows = jnp.concatenate(
        [pieces[:, :, j : j + n_chaos] for j in range(2 * side + 1)], axis=-1
    )
    sent = jnp.transpose(windows[:cap], (2, 0, 1, 3))
    got = lax.all_to_all(sent, "chaos", 0, 0, tiled=True)
    by_slot = got.reshape(n_chaos * cap, cells)
    my_fields = lax.dynamic_index_in_dim(windows[cap:], my_col_block, axis=2, keepdims=False)
    my_fields = my_fields.reshape(M + 1, cells)

    blocks, row_of, total = coupling_blocks(M)
    sizes, firsts, padded, offsets = degree_layout(M)
    coeff_of_row = np.full(total, -1, np.int64)
    coeff_of_row[row_of] = np.arange(count)
    row_coeff = jnp.asarray(np.maximum(coeff_of_row, 0), jnp.int32)
    group_ends = jnp.cumsum(lengths).astype(jnp.int32)
    group_starts = (group_ends - lengths).astype(jnp.int32)
    skipped = jnp.sum(
        jnp.where(row_coeff[:, None] >= group_ends[None, :], cap - lengths[None, :], 0), axis=1
    )
    slot_of_row = jnp.where(jnp.asarray(coeff_of_row >= 0), row_coeff + skipped, n_chaos * cap)
    by_slot = jnp.concatenate([by_slot, jnp.zeros((1, cells), jnp.float32)], axis=0)
    rhs = jnp.take(by_slot, slot_of_row, axis=0)

    row_at = my_row_block * rows - ghost + jnp.arange(patch_rows)
    col_at = my_col_block * width - ghost + jnp.arange(patch_cols)
    inside = ((row_at >= 0) & (row_at < rows * n_space))[:, None] & (
        (col_at >= 0) & (col_at < cols)
    )[None, :]
    inside = inside.reshape(cells)
    local_rows = jnp.arange(patch_rows)
    local_cols = jnp.arange(patch_cols)
    own = ((local_rows >= ghost) & (local_rows < ghost + rows))[:, None] & (
        (local_cols >= ghost) & (local_cols < ghost + width)
    )[None, :]
    own = own.reshape(cells)

    lanes = -(-cells // 128) * 128
    assert cells + patch_cols <= lanes
    rhs = jnp.pad(rhs, ((0, 0), (0, lanes - cells)))
    field_rows = -(-(M + 1) // 8) * 8
    field_in = jnp.pad(my_fields, ((0, field_rows - (M + 1)), (0, lanes - cells)))
    masks = jnp.stack([inside, own]).astype(jnp.float32)
    masks = jnp.pad(masks, ((0, 6), (0, lanes - cells)))
    mats = [jnp.asarray(blocks[d]) for d in range(4)]
    solved, partial_rows = pl.pallas_call(
        functools.partial(sweeps, padded=tuple(int(v) for v in padded), offsets=tuple(int(v) for v in offsets), cols=patch_cols),
        out_shape=(
            jax.ShapeDtypeStruct((total, lanes), jnp.float32),
            jax.ShapeDtypeStruct((8, 128), jnp.float32),
        ),
        in_specs=[pl.BlockSpec(memory_space=pltpu.VMEM)] * 7,
        out_specs=(pl.BlockSpec(memory_space=pltpu.VMEM), pl.BlockSpec(memory_space=pltpu.VMEM)),
        scratch_shapes=[pltpu.VMEM((M * padded[d], lanes), jnp.float32) for d in range(4)],
        compiler_params=pltpu.CompilerParams(vmem_limit_bytes=48 * 1024 * 1024),
    )(rhs, field_in, masks, *mats)
    partials = partial_rows[0, :ITERS]

    mine = solved[:, :cells].reshape(total, patch_rows, patch_cols)[
        :, ghost : ghost + rows, ghost : ghost + width
    ]
    mine = jnp.concatenate([mine, jnp.zeros((1, rows, width), jnp.float32)], axis=0)
    slot_index = jnp.arange(cap, dtype=jnp.int32)
    live = slot_index[None, :] < lengths[:, None]
    coeff = group_starts[:, None] + slot_index[None, :]
    shift = jnp.zeros_like(coeff)
    for d in range(1, 4):
        shift = jnp.where(coeff >= firsts[d], int(offsets[d] - firsts[d]), shift)
    row_of_slot = jnp.where(live, coeff + shift, total)
    by_slot_out = jnp.take(mine, row_of_slot.reshape(-1), axis=0)
    chunk = cap * rows * width
    payload = jnp.concatenate(
        [
            by_slot_out.reshape(n_chaos, chunk),
            jnp.broadcast_to(partials[None, :], (n_chaos, ITERS)),
        ],
        axis=1,
    )
    back = lax.all_to_all(payload, "chaos", 0, 0, tiled=True)
    out = back[:, :chunk].reshape(n_chaos, cap, rows, width)
    out = jnp.transpose(out, (1, 2, 0, 3)).reshape(cap, rows, cols)
    row_sum = jnp.sum(back[:, chunk:], axis=0)
    spread = jnp.broadcast_to(row_sum[None, :], (n_space, ITERS))
    all_rows = lax.all_to_all(spread, "space", 0, 0, tiled=True)
    norms = jnp.sqrt(jnp.sum(all_rows, axis=0))
    return (out, norms)


def solution(mesh):
    in_specs = (P("chaos", "space", None), P("space", None), P(None, "space", None), P())
    out_specs = (P("chaos", "space", None), P())
    return jax.shard_map(local, mesh=mesh, in_specs=in_specs, out_specs=out_specs, check_vma=False)
```

profile of v0, /device:TPU:1, one launch (start us, length us, event | category | flops | bytes accessed | tf_op | source)
XLA Modules:
  0.0 137.7 jit_solution(5503288602276180662)
XLA Ops:
  0.6 0.7 broadcast.222
  1.3 0.7 broadcast_multiply_fusion
  2.1 0.9 pad_maximum_fusion.2
  2.9 4.4 %collective-permute-start = (f32[43,4,128]{2,1,0:T(4,128)S(1)}, f32[43,4,128]{2,1,0:T(4,128)S(1)}, u32[]{:S(2)}, u32[]{:S(2)}) collective-permute-start(f32[43,4,128]{2,1,0:T(4,128)S(1)} %pad_maximum_fusion.2), channel_id=1, source_target_pairs={{0,32},{32,64},{64,96},{96,128},{128,160},{160,192},{192,224},{224... | collective-permute-start | bytes 264200 | tf_op jit(solution)/shard_map/ppermute | solution.py:201
  7.3 1.3 collective-permute-start.1
  8.6 0.7 iota_compare_fusion
  9.3 0.7 copy.73
  10.1 0.1 reduce-window.8
  10.1 0.1 reduce.1
  10.3 0.7 fusion.3
  10.9 0.1 iota_add_fusion
  11.0 0.1 add.124
  11.1 0.1 add.112
  11.2 0.1 lt.98
  11.3 0.1 lt.89
  11.4 0.8 select_reduce_fusion
  12.2 0.7 compare_select_fusion.5
  12.9 0.1 broadcast_and_fusion.1
  13.0 0.1 and.93
  13.1 0.1 broadcast_and_fusion
  13.2 0.1 and.98
  13.4 0.0 collective-permute-done
  13.4 0.0 collective-permute-done.1
  13.4 0.9 pad_maximum_fusion.1
  14.3 0.3 copy.88
  14.6 0.1 pad.20.clone
  14.7 0.3 fusion.2
  15.0 0.7 pad_maximum_fusion
  15.8 2.1 %copy_bitcast_fusion = f32[32,12,12,30]{3,2,1,0:T(8,128)} fusion(f32[43,12,32,12]{0,3,2,1:T(8,128)S(1)} %pad_maximum_fusion), kind=kLoop, calls=%fused_computation.39 | loop fusion | bytes 1345536
  17.8 4.2 %reshape.259 = f32[32,1,4320]{2,1,0:T(1,128)} reshape(f32[32,12,12,30]{3,2,1,0:T(8,128)} %copy_bitcast_fusion) | data formatting | bytes 1105920
  22.0 8.4 %all-to-all-start = ((f32[32,1,4320]{2,1,0:T(1,128)}), f32[32,1,4320]{2,1,0:T(1,128)}, u32[]{:S(2)}, u32[]{:S(2)}) async-start(f32[32,1,4320]{2,1,0:T(1,128)} %reshape.259), calls=%async_computation | async-start | bytes 1114112 | tf_op jit(solution)/shard_map/all_to_all | solution.py:212
  30.5 0.0 copy-done.4
  30.5 0.9 slice.48
  31.4 0.1 copy.86
  31.5 10.9 %all-to-all-done = f32[32,1,4320]{2,1,0:T(1,128)} async-done(((f32[32,1,4320]{2,1,0:T(1,128)}), f32[32,1,4320]{2,1,0:T(1,128)}, u32[]{:S(2)}, u32[]{:S(2)}) %all-to-all-start) | async-done | bytes 552992 | tf_op jit(solution)/shard_map/all_to_all | solution.py:212
  42.4 0.5 broadcast.223
  42.9 3.8 %reduce.2 = f32[32,4320]{1,0:T(8,128)} reduce(f32[32,1,4320]{2,1,0:T(1,128)} %all-to-all-done, f32[]{:T(128)} %broadcast.223), dimensions={1}, to_apply=%all_to_all.15.reduce_sub_computation | reduce | bytes 1105924 | tf_op jit(solution)/shard_map/all_to_all | solution.py:212
  46.8 2.8 %reshape.260 = f32[32,12,12,30]{3,2,1,0:T(8,128)S(1)} reshape(f32[32,4320]{1,0:T(8,128)} %reduce.2) | data formatting | bytes 1105920
  49.5 2.8 %copy.76 = f32[32,30,12,12]{1,0,3,2:T(8,128)} copy(f32[32,30,12,12]{1,3,2,0:T(8,128)S(1)} %bitcast.30) | data formatting | bytes 1105920 | tf_op jit(solution)/shard_map/all_to_all | solution.py:212
  52.3 3.0 %reshape.233 = f32[960,144]{0,1:T(8,128)S(1)} reshape(f32[32,30,12,12]{1,0,3,2:T(8,128)} %copy.76) | data formatting | bytes 1105920 | tf_op jit(solution)/shard_map/reshape | solution.py:213
  55.3 0.3 copy.77
  55.6 1.0 concatenate.21
  56.6 3.6 %gather_fusion = f32[472,144]{1,0:T(8,128)} fusion(f32[961,144]{1,0:T(8,128)} %concatenate.21, s32[1024]{0:T(1024)S(1)} %pad_clamp_fusion.1), kind=kCustom, calls=%fused_computation | custom fusion | bytes 545632 | tf_op jit(solution)/shard_map/jit(_take)/gather | solution.py:229
  60.2 1.2 broadcast_select_fusion.1
  61.4 0.0 copy-start.2
  61.4 0.9 copy-done.2
  62.3 18.8 %shard_map.113 = (f32[472,256]{1,0:T(8,128)S(1)}, f32[8,128]{1,0:T(8,128)S(1)}) custom-call(f32[472,256]{1,0:T(8,128)S(1)} %pad.21.rhs_ref, f32[16,256]{1,0:T(8,128)S(1)} %pad.22.field_ref, f32[8,256]{1,0:T(8,128)S(1)} %pad_convert_fusion.mask_ref, f32[16,96]{1,0:T(8,128)S(1)} %copy-done.3, f32[88,192]{1,0:T(8,128)S(1)} %copy-done.2, ...), custom_call_target="tpu_custom_call" | custom-call | tf_op jit(solution)/shard_map/pallas_call | solution.py:252
  81.1 3.6 %reshape.256 = f32[472,12,12]{2,1,0:T(8,128)} reshape(f32[472,144]{1,0:T(8,128)S(1)} %bitcast.29) | data formatting | bytes 543744 | tf_op jit(solution)/shard_map/reshape | solution.py:265
  84.7 2.1 %slice.49 = f32[472,4,4]{2,1,0:T(4,128)S(1)} slice(f32[472,12,12]{2,1,0:T(8,128)} %reshape.256), slice={[0:472], [4:8], [4:8]} | slice | bytes 60416 | tf_op jit(solution)/shard_map/slice | solution.py:265
  86.8 0.2 concatenate.22
  87.0 3.5 %gather_fusion.1 = f32[960,4,4]{2,1,0:T(4,128)S(1)} fusion(f32[473,4,4]{2,1,0:T(4,128)S(1)} %concatenate.22, s32[1024]{0:T(1024)S(1)} %pad_clamp_fusion), kind=kCustom, calls=%fused_computation.1 | custom fusion | bytes 126720 | tf_op jit(solution)/shard_map/jit(_take)/gather | solution.py:276
  90.5 4.3 %broadcast_select_fusion = f32[960,4,4]{2,1,0:T(4,128)} fusion(f32[960,4,4]{2,1,0:T(4,128)S(1)} %gather_fusion.1, pred[960]{0:T(1024)(128)(4,1)S(1)} %compare_and_fusion), kind=kLoop, calls=%fused_computation.4 | loop fusion | flops 15360 | bytes 123840 | tf_op jit(solution)/shard_map/jit(_take)/select_n | solution.py:276
  94.8 2.6 %select_n.123 = f32[32,480]{1,0:T(8,128)S(1)} reshape(f32[960,4,4]{2,1,0:T(4,128)} %broadcast_select_fusion) | data formatting | bytes 122880 | tf_op jit(solution)/shard_map/jit(_take)/select_n | solution.py:276
  97.4 0.1 pad.26.clone
  97.5 0.1 copy.81
  97.6 10.8 %all_to_all.23 = f32[32,1,483]{2,1,0:T(1,128)S(1)} all-to-all(f32[32,1,483]{2,1,0:T(1,128)S(1)} %copy.81), channel_id=1, replica_groups=mesh['space'=16,'chaos'=32] {'chaos'}, dimensions={0} | all-to-all | bytes 123648 | tf_op jit(solution)/shard_map/all_to_all | solution.py:285
  108.4 0.1 copy.82
  108.5 0.1 slice_reduce_fusion
  108.6 0.6 broadcast_in_dim.115
  109.2 16.5 %all-to-all-start.2 = ((f32[16,1,3]{2,1,0:T(1,128)}), f32[16,1,3]{2,1,0:T(1,128)S(1)}, u32[]{:S(2)}, u32[]{:S(2)}) async-start(f32[16,1,3]{2,1,0:T(1,128)} %broadcast_in_dim.115), calls=%async_computation.2 | async-start | bytes 16384 | tf_op jit(solution)/shard_map/all_to_all | solution.py:290
  125.8 0.2 copy.83
  126.0 0.7 copy.85
  126.8 10.4 %all-to-all-done.2 = f32[16,1,3]{2,1,0:T(1,128)S(1)} async-done(((f32[16,1,3]{2,1,0:T(1,128)}), f32[16,1,3]{2,1,0:T(1,128)S(1)}, u32[]{:S(2)}, u32[]{:S(2)}) %all-to-all-start.2) | async-done | bytes 224 | tf_op jit(solution)/shard_map/all_to_all | solution.py:290
  137.2 0.5 sqrt.3
  (26 shorter events, 0.2 us)
Async XLA Ops:
  2.9 10.4 %collective-permute-start = (f32[43,4,128]{2,1,0:T(4,128)S(1)}, f32[43,4,128]{2,1,0:T(4,128)S(1)}, u32[]{:S(2)}, u32[]{:S(2)}) collective-permute-start(f32[43,4,128]{2,1,0:T(4,128)S(1)} %pad_maximum_fusion.2), channel_id=1, source_target_pairs={{0,32},{32,64},{64,96},{96,128},{128,160},{160,192},{192,224},{224... | collective-permute-start | bytes 264200 | tf_op jit(solution)/shard_map/ppermute | solution.py:201
  7.3 6.1 %collective-permute-start.1 = (f32[43,4,128]{2,1,0:T(4,128)S(1)}, f32[43,4,128]{2,1,0:T(4,128)S(1)}, u32[]{:S(2)}, u32[]{:S(2)}) collective-permute-start(f32[43,4,128]{2,1,0:T(4,128)S(1)} %pad_maximum_fusion.2), channel_id=1, source_target_pairs={{32,0},{64,32},{96,64},{128,96},{160,128},{192,160},{224,192},{256... | collective-permute-start | bytes 264200 | tf_op jit(solution)/shard_map/ppermute | solution.py:202
  17.8 12.6 %copy-start.4 = (s32[472]{0:T(512)S(1)}, s32[472]{0:T(512)}, u32[]{:S(2)}) copy-start(s32[472]{0:T(512)} %constant.96.clone) | copy-start | bytes 5668
  17.8 12.6 %copy-start.5 = (pred[472]{0:T(512)(128)(4,1)S(1)}, pred[472]{0:T(512)(128)(4,1)}, u32[]{:S(2)}) copy-start(pred[472]{0:T(512)(128)(4,1)} %constant.97.clone) | copy-start | bytes 1420
  22.0 20.4 %all-to-all-start = ((f32[32,1,4320]{2,1,0:T(1,128)}), f32[32,1,4320]{2,1,0:T(1,128)}, u32[]{:S(2)}, u32[]{:S(2)}) async-start(f32[32,1,4320]{2,1,0:T(1,128)} %reshape.259), calls=%async_computation | async-start | bytes 1114112 | tf_op jit(solution)/shard_map/all_to_all | solution.py:212
  56.6 4.8 %copy-start = (f32[384,960]{1,0:T(8,128)S(1)}, f32[384,960]{1,0:T(8,128)}, u32[]{:S(2)}) copy-start(f32[384,960]{1,0:T(8,128)} %constant.100.clone.w2_ref) | copy-start | bytes 4423684
  56.6 4.8 %copy-start.1 = (f32[80,4416]{1,0:T(8,128)S(1)}, f32[80,4416]{1,0:T(8,128)}, u32[]{:S(2)}) copy-start(f32[80,4416]{1,0:T(8,128)} %constant.101.clone.w3_ref) | copy-start | bytes 4239364
  56.6 4.8 %copy-start.3 = (f32[16,96]{1,0:T(8,128)S(1)}, f32[16,96]{1,0:T(8,128)}, u32[]{:S(2)}) copy-start(f32[16,96]{1,0:T(8,128)} %constant.98.clone.w0_ref) | copy-start | bytes 18436
  61.4 0.9 copy-start.2
  109.2 27.9 %all-to-all-start.2 = ((f32[16,1,3]{2,1,0:T(1,128)}), f32[16,1,3]{2,1,0:T(1,128)S(1)}, u32[]{:S(2)}, u32[]{:S(2)}) async-start(f32[16,1,3]{2,1,0:T(1,128)} %broadcast_in_dim.115), calls=%async_computation.2 | async-start | bytes 16384 | tf_op jit(solution)/shard_map/all_to_all | solution.py:290
where the time goes:
time: 138 us
  local copies, waits for them, and re-layouts  39.2 us (28%)
  starting transfers between devices  30.6 us (22%)
  waiting for transfers between devices  21.3 us (15%)
  Pallas kernels  18.8 us (14%)
  other arithmetic  16 us (12%)
  blocking collectives  10.8 us (8%)
    pallas_call x1, Pallas kernels, local(): pl.pallas_call(functools.partial(sweeps, padded=tuple((int(v) for v in pa...  18.8 us
    all_to_all x1, starting transfers between devices, local(): all_rows = lax.all_to_all(spread, 'space', 0, 0, tiled=True)  16.5 us
    unnamed x18, local copies, waits for them, and re-layouts  11.7 us
    all_to_all x1, waiting for transfers between devices, local(): got = lax.all_to_all(sent, 'chaos', 0, 0, tiled=True)  10.9 us
    all_to_all x1, blocking collectives, local(): back = lax.all_to_all(payload, 'chaos', 0, 0, tiled=True)  10.8 us
    all_to_all x1, waiting for transfers between devices, local(): all_rows = lax.all_to_all(spread, 'space', 0, 0, tiled=True)  10.4 us
    all_to_all x1, starting transfers between devices, local(): got = lax.all_to_all(sent, 'chaos', 0, 0, tiled=True)  8.4 us
    ppermute x1, starting transfers between devices, local(): above = lax.ppermute(block[:, rows - ghost:], 'space', down_pairs)  4.36 us
  transfers between devices with their start and end apart: 4, of which 2 were waited for; matrix products, arithmetic and copies ran while one was open for 5% of the time, Pallas kernels for 0%

commit v1 on v0

--- a/solution.py
+++ b/solution.py
@@ -116,9 +116,18 @@
     return jnp.concatenate([blank, values[..., :step]], axis=-1)
 
 
-def sweeps(rhs_ref, field_ref, mask_ref, w0_ref, w1_ref, w2_ref, w3_ref, sol_ref, part_ref,
-           s0_ref, s1_ref, s2_ref, s3_ref, *, padded, offsets, cols):
-    lanes = rhs_ref.shape[1]
+def exact_dot(left, right):
+    return jnp.dot(left, right, precision=lax.Precision.HIGHEST, preferred_element_type=jnp.float32)
+
+
+def sweeps(slots_ref, slot_of_row_ref, row_of_slot_ref, picks_ref, field_ref, mask_ref,
+           w0_ref, w1_ref, w2_ref, w3_ref, out_ref, part_ref,
+           s0_ref, s1_ref, s2_ref, s3_ref, *, padded, offsets, cols, state_rows):
+    lanes = slots_ref.shape[1]
+    total = slot_of_row_ref.shape[0]
+    n_slots = slots_ref.shape[0]
+    take = lax.broadcasted_iota(jnp.int32, (total, n_slots), 1) == slot_of_row_ref[...]
+    rhs = exact_dot(take.astype(jnp.float32), slots_ref[...])
     shifts = (cols, lanes - cols, lanes - 1, 1)
 
     def near(values, shift):
@@ -149,7 +158,7 @@
             for d in range(4):
                 stacks[d][(k - 1) * padded[d] : k * padded[d], :] = term[offsets[d] : offsets[d] + padded[d]]
         mixed = [
-            jnp.dot(mats[d][...], stacks[d][...], precision=lax.Precision.HIGHEST, preferred_element_type=jnp.float32)
+            exact_dot(mats[d][...], stacks[d][...])
             for d in range(4)
         ]
         p0, p1 = padded[0], padded[1]
@@ -162,7 +171,7 @@
     delta = (spectrum_high - spectrum_low) / 2.0
     sigma = theta / delta
     rho = 1.0 / sigma
-    residual = rhs_ref[...]
+    residual = rhs
     solution = jnp.zeros_like(residual)
     direction = jnp.where(inside, residual / diagonal / theta, 0.0)
     lane = lax.broadcasted_iota(jnp.int32, (8, 128), 1)
@@ -177,7 +186,12 @@
             direction = rho_new * rho * direction + 2.0 * rho_new / delta * (residual / diagonal)
             direction = jnp.where(inside, direction, 0.0)
             rho = rho_new
-    sol_ref[...] = solution
+    own_cells = exact_dot(solution, picks_ref[...])
+    own_cells = jnp.concatenate(
+        [own_cells, jnp.zeros((state_rows - total, own_cells.shape[1]), jnp.float32)], axis=0
+    )
+    put = lax.broadcasted_iota(jnp.int32, (n_slots, state_rows), 1) == row_of_slot_ref[...]
+    out_ref[...] = exact_dot(put.astype(jnp.float32), own_cells)
     part_ref[...] = partial_out
 
 
@@ -208,9 +222,13 @@
     windows = jnp.concatenate(
         [pieces[:, :, j : j + n_chaos] for j in range(2 * side + 1)], axis=-1
     )
-    sent = jnp.transpose(windows[:cap], (2, 0, 1, 3))
+    lanes = -(-cells // 128) * 128
+    assert cells + patch_cols <= lanes
+    slot_rows = -(-(cap + 1) // 8) * 8
+    sent = jnp.transpose(windows[:cap], (2, 0, 1, 3)).reshape(n_chaos, cap, cells)
+    sent = jnp.pad(sent, ((0, 0), (0, slot_rows - cap), (0, lanes - cells)))
     got = lax.all_to_all(sent, "chaos", 0, 0, tiled=True)
-    by_slot = got.reshape(n_chaos * cap, cells)
+    by_slot = got.reshape(n_chaos * slot_rows, lanes)
     my_fields = lax.dynamic_index_in_dim(windows[cap:], my_col_block, axis=2, keepdims=False)
     my_fields = my_fields.reshape(M + 1, cells)
 
@@ -222,11 +240,18 @@
     group_ends = jnp.cumsum(lengths).astype(jnp.int32)
     group_starts = (group_ends - lengths).astype(jnp.int32)
     skipped = jnp.sum(
-        jnp.where(row_coeff[:, None] >= group_ends[None, :], cap - lengths[None, :], 0), axis=1
-    )
-    slot_of_row = jnp.where(jnp.asarray(coeff_of_row >= 0), row_coeff + skipped, n_chaos * cap)
-    by_slot = jnp.concatenate([by_slot, jnp.zeros((1, cells), jnp.float32)], axis=0)
-    rhs = jnp.take(by_slot, slot_of_row, axis=0)
+        jnp.where(row_coeff[:, None] >= group_ends[None, :], slot_rows - lengths[None, :], 0), axis=1
+    )
+    slot_of_row = jnp.where(
+        jnp.asarray(coeff_of_row >= 0), row_coeff + skipped, n_chaos * slot_rows - 1
+    ).astype(jnp.int32)
+    slot_index = jnp.arange(slot_rows, dtype=jnp.int32)
+    live = slot_index[None, :] < lengths[:, None]
+    coeff = group_starts[:, None] + slot_index[None, :]
+    shift = jnp.zeros_like(coeff)
+    for d in range(1, 4):
+        shift = jnp.where(coeff >= firsts[d], int(offsets[d] - firsts[d]), shift)
+    row_of_slot = jnp.where(live, coeff + shift, -1).astype(jnp.int32).reshape(-1)
 
     row_at = my_row_block * rows - ghost + jnp.arange(patch_rows)
     col_at = my_col_block * width - ghost + jnp.arange(patch_cols)
@@ -241,39 +266,36 @@
     )[None, :]
     own = own.reshape(cells)
 
-    lanes = -(-cells // 128) * 128
-    assert cells + patch_cols <= lanes
-    rhs = jnp.pad(rhs, ((0, 0), (0, lanes - cells)))
     field_rows = -(-(M + 1) // 8) * 8
     field_in = jnp.pad(my_fields, ((0, field_rows - (M + 1)), (0, lanes - cells)))
     masks = jnp.stack([inside, own]).astype(jnp.float32)
     masks = jnp.pad(masks, ((0, 6), (0, lanes - cells)))
     mats = [jnp.asarray(blocks[d]) for d in range(4)]
+    own_lanes = np.flatnonzero(np.pad(np.ones((rows, width)), ghost).reshape(-1) > 0.5)
+    picks = np.zeros((lanes, 128), np.float32)
+    picks[own_lanes, np.arange(own_lanes.size)] = 1.0
+    state_rows = -(-total // 128) * 128
     solved, partial_rows = pl.pallas_call(
-        functools.partial(sweeps, padded=tuple(int(v) for v in padded), offsets=tuple(int(v) for v in offsets), cols=patch_cols),
+        functools.partial(
+            sweeps,
+            padded=tuple(int(v) for v in padded),
+            offsets=tuple(int(v) for v in offsets),
+            cols=patch_cols,
+            state_rows=state_rows,
+        ),
         out_shape=(
-            jax.ShapeDtypeStruct((total, lanes), jnp.float32),
+            jax.ShapeDtypeStruct((n_chaos * slot_rows, 128), jnp.float32),
             jax.ShapeDtypeStruct((8, 128), jnp.float32),
         ),
-        in_specs=[pl.BlockSpec(memory_space=pltpu.VMEM)] * 7,
+        in_specs=[pl.BlockSpec(memory_space=pltpu.VMEM)] * 10,
         out_specs=(pl.BlockSpec(memory_space=pltpu.VMEM), pl.BlockSpec(memory_space=pltpu.VMEM)),
         scratch_shapes=[pltpu.VMEM((M * padded[d], lanes), jnp.float32) for d in range(4)],
         compiler_params=pltpu.CompilerParams(vmem_limit_bytes=48 * 1024 * 1024),
-    )(rhs, field_in, masks, *mats)
+    )(by_slot, slot_of_row[:, None], row_of_slot[:, None], jnp.asarray(picks), field_in, masks, *mats)
     partials = partial_rows[0, :ITERS]
 
-    mine = solved[:, :cells].reshape(total, patch_rows, patch_cols)[
-        :, ghost : ghost + rows, ghost : ghost + width
-    ]
-    mine = jnp.concatenate([mine, jnp.zeros((1, rows, width), jnp.float32)], axis=0)
-    slot_index = jnp.arange(cap, dtype=jnp.int32)
-    live = slot_index[None, :] < lengths[:, None]
-    coeff = group_starts[:, None] + slot_index[None, :]
-    shift = jnp.zeros_like(coeff)
-    for d in range(1, 4):
-        shift = jnp.where(coeff >= firsts[d], int(offsets[d] - firsts[d]), shift)
-    row_of_slot = jnp.where(live, coeff + shift, total)
-    by_slot_out = jnp.take(mine, row_of_slot.reshape(-1), axis=0)
+    own_count = rows * width
+    by_slot_out = solved[:, :own_count].reshape(n_chaos, slot_rows, own_count)[:, :cap]
     chunk = cap * rows * width
     payload = jnp.concatenate(
         [

time: 138 us -> 117 us (0.85)
  local copies, waits for them, and re-layouts: 39.2 us -> 24.7 us
  other arithmetic: 16 us -> 6.22 us
  Pallas kernels: 18.8 us -> 24.5 us
  waiting for transfers between devices: 21.3 us -> 18.8 us
    gather x2 -> x0, local copies, waits for them, and re-layouts: 7.12 us -> none  [the longest x1 3.58 us: local(): rhs = jnp.take(by_slot, slot_of_row, axis=0)]
    reshape x3 -> x1, local copies, waits for them, and re-layouts: 6.86 us -> 0.1 us  [local(): by_slot_out.reshape(n_chaos, chunk)]
    pallas_call x1, Pallas kernels: 18.8 us -> 24.5 us  [local(): pl.pallas_call(functools.partial(sweeps, padded=tuple((int(v) for v in pa...]
    select_n x4 -> x2, other arithmetic: 6.16 us -> 0.88 us  [the longest x1 0.71 us: local(): jnp.where(jnp.asarray(coeff_of_row >= 0), row_coeff + skipped, n_chaos *...]
    all_to_all x2 -> x0, other arithmetic: 3.83 us -> none  [the longest x1 3.82 us: local(): got = lax.all_to_all(sent, 'chaos', 0, 0, tiled=True)]
    all_to_all x2 -> x0, local copies, waits for them, and re-layouts: 3.29 us -> none  [local(): got = lax.all_to_all(sent, 'chaos', 0, 0, tiled=True)]
    all_to_all x1, waiting for transfers between devices: 10.9 us -> 7.84 us  [local(): got = lax.all_to_all(sent, 'chaos', 0, 0, tiled=True)]
    reshape x2, local copies, waits for them, and re-layouts: 0.08 us -> 3.1 us  [local(): my_fields = my_fields.reshape(M + 1, cells)]
  transfers between devices with their start and end apart: 4 -> 4, of which waited for: 2 -> 3; matrix products, arithmetic and copies ran while one was open for 5% -> 11% of each run, Pallas kernels for 0% -> 0%
where the time goes in v1:
time: 117 us; the launch traced here: 116 us
  starting transfers between devices  30.2 us (26%)
  local copies, waits for them, and re-layouts  24.7 us (21%)
  Pallas kernels  24.5 us (21%)
  waiting for transfers between devices  18.8 us (16%)
  blocking collectives  11.1 us (9%)
  other arithmetic  6.22 us (5%)
    pallas_call x1, Pallas kernels, local(): pl.pallas_call(functools.partial(sweeps, padded=tuple((int(v) for v in pa...  24.5 us
    all_to_all x1, starting transfers between devices, local(): all_rows = lax.all_to_all(spread, 'space', 0, 0, tiled=True)  15.3 us
    all_to_all x1, blocking collectives, local(): back = lax.all_to_all(payload, 'chaos', 0, 0, tiled=True)  11.1 us
    all_to_all x1, waiting for transfers between devices, local(): all_rows = lax.all_to_all(spread, 'space', 0, 0, tiled=True)  10.4 us
    unnamed x21, local copies, waits for them, and re-layouts  9.81 us
    all_to_all x1, starting transfers between devices, local(): got = lax.all_to_all(sent, 'chaos', 0, 0, tiled=True)  9.19 us
    all_to_all x1, waiting for transfers between devices, local(): got = lax.all_to_all(sent, 'chaos', 0, 0, tiled=True)  7.84 us
    ppermute x1, starting transfers between devices, local(): above = lax.ppermute(block[:, rows - ghost:], 'space', down_pairs)  4.36 us
  transfers between devices with their start and end apart: 4, of which 3 were waited for; matrix products, arithmetic and copies ran while one was open for 11% of the time, Pallas kernels for 0%

profile of v1, /device:TPU:1, one launch (start us, length us, event | category | flops | bytes accessed | tf_op | source)
XLA Modules:
  0.0 116.3 jit_solution(15407560848874277529)
XLA Ops:
  0.6 0.7 broadcast.158
  1.3 0.7 broadcast_multiply_fusion
  2.1 0.9 pad_maximum_fusion.2
  2.9 4.4 %collective-permute-start = (f32[43,4,128]{2,1,0:T(4,128)S(1)}, f32[43,4,128]{2,1,0:T(4,128)S(1)}, u32[]{:S(2)}, u32[]{:S(2)}) collective-permute-start(f32[43,4,128]{2,1,0:T(4,128)S(1)} %pad_maximum_fusion.2), channel_id=1, source_target_pairs={{0,32},{32,64},{64,96},{96,128},{128,160},{160,192},{192,224},{224... | collective-permute-start | bytes 264200 | tf_op jit(solution)/shard_map/ppermute | solution.py:215
  7.3 1.3 %collective-permute-start.1 = (f32[43,4,128]{2,1,0:T(4,128)S(1)}, f32[43,4,128]{2,1,0:T(4,128)S(1)}, u32[]{:S(2)}, u32[]{:S(2)}) collective-permute-start(f32[43,4,128]{2,1,0:T(4,128)S(1)} %pad_maximum_fusion.2), channel_id=1, source_target_pairs={{32,0},{64,32},{96,64},{128,96},{160,128},{192,160},{224,192},{256... | collective-permute-start | bytes 264200 | tf_op jit(solution)/shard_map/ppermute | solution.py:216
  8.6 0.1 broadcast_and_fusion
  8.7 0.7 copy.83
  9.4 0.1 reduce-window.8
  9.5 0.1 reduce.1
  9.6 0.7 fusion.1
  10.3 0.8 select_reduce_fusion
  11.0 0.7 add_select_fusion.1
  11.8 0.1 broadcast_and_fusion.1
  11.8 0.1 and.79
  11.9 0.1 and.84
  12.0 0.1 copy.90.slot_of_row_ref
  12.2 0.0 collective-permute-done
  12.2 0.6 collective-permute-done.1
  12.7 0.9 pad_maximum_fusion.1
  13.6 0.3 copy.100
  13.9 0.1 pad.18.clone
  14.0 0.3 fusion
  14.4 0.7 pad_maximum_fusion
  15.1 0.0 copy-start.6
  15.1 0.2 slice_bitcast_fusion
  15.3 1.4 %copy-done.6 = f32[43,12,32,12]{0,3,2,1:T(8,128)} copy-done((f32[43,12,32,12]{0,3,2,1:T(8,128)}, f32[43,12,32,12]{0,3,2,1:T(8,128)S(1)}, u32[]{:S(2)}) %copy-start.6) | copy-done | bytes 792600
  16.7 0.7 copy.81
  17.5 2.3 %copy.101 = f32[32,30,144]{2,1,0:T(8,128)} copy(f32[32,30,144]{1,0,2:T(8,128)S(1)} %bitcast.27) | data formatting | bytes 1105920
  19.8 2.3 %pad.19.clone = f32[32,32,256]{2,1,0:T(8,128)} pad(f32[32,30,144]{2,1,0:T(8,128)} %copy.101, f32[]{:T(128)} %constant.26.clone.1), padding=0_0x0_2x0_112 | pad | bytes 1601540 | tf_op jit(solution)/shard_map/jit(_pad)/pad | solution.py:229
  22.1 9.2 %all-to-all-start = ((f32[32,32,256]{2,1,0:T(8,128)}), f32[32,32,256]{2,1,0:T(8,128)S(1)}, u32[]{:S(2)}, u32[]{:S(2)}) async-start(f32[32,32,256]{2,1,0:T(8,128)} %pad.19.clone), calls=%async_computation | async-start | bytes 2097152 | tf_op jit(solution)/shard_map/all_to_all | solution.py:230
  31.3 0.1 iota_add_fusion
  31.4 0.5 add.77
  31.9 0.1 iota_compare_fusion
  32.0 0.6 lt.64
  32.6 0.2 add_select_fusion.row_of_slot_ref
  32.8 0.0 copy-start
  32.8 0.0 copy-start.3
  32.8 0.0 copy-start.5
  32.8 2.9 %slice.44 = f32[13,12,32,12]{0,3,2,1:T(8,128)S(1)} slice(f32[43,12,32,12]{0,3,2,1:T(8,128)} %copy-done.6), slice={[30:43], [0:12], [0:32], [0:12]} | slice | bytes 479232 | tf_op jit(solution)/shard_map/slice | solution.py:232
  35.7 0.6 constant_dynamic-slice_fusion
  36.4 1.5 %reshape.216 = f32[13,144]{0,1:T(8,128)} reshape(f32[13,12,1,12]{0,3,2,1:T(8,128)} %constant_dynamic-slice_fusion) | data formatting | bytes 14976 | tf_op jit(solution)/shard_map/reshape | solution.py:233
  37.9 1.6 %copy.97 = f32[13,144]{1,0:T(8,128)} copy(f32[13,144]{0,1:T(8,128)} %reshape.216) | data formatting | bytes 14976 | tf_op jit(solution)/shard_map/reshape | solution.py:233
  39.5 0.7 pad.20.field_ref
  40.2 7.8 %all-to-all-done = f32[32,32,256]{2,1,0:T(8,128)S(1)} async-done(((f32[32,32,256]{2,1,0:T(8,128)}), f32[32,32,256]{2,1,0:T(8,128)S(1)}, u32[]{:S(2)}, u32[]{:S(2)}) %all-to-all-start) | async-done | bytes 1048608 | tf_op jit(solution)/shard_map/all_to_all | solution.py:230
  48.0 0.0 copy-done
  48.0 0.0 copy-done.5
  48.0 0.0 copy-start.1
  48.1 1.4 %copy-done.1 = f32[80,4416]{1,0:T(8,128)S(1)} copy-done((f32[80,4416]{1,0:T(8,128)S(1)}, f32[80,4416]{1,0:T(8,128)}, u32[]{:S(2)}) %copy-start.1) | copy-done | bytes 1413144
  49.4 0.9 copy-done.4
  50.3 24.5 %shard_map.122 = (f32[1024,128]{1,0:T(8,128)S(1)}, f32[8,128]{1,0:T(8,128)S(1)}) custom-call(f32[1024,256]{1,0:T(8,128)S(1)} %bitcast.24, s32[472,1]{1,0:T(8,128)S(1)} %copy.90.slot_of_row_ref, s32[1024,1]{1,0:T(8,128)S(1)} %add_select_fusion.row_of_slot_ref, f32[256,128]{1,0:T(8,128)S(1)} %copy-done.3, f32[16,256]{1,0:T(8,128)S(1)} %pad.20.field_ref, ...), custom_call_target="tpu_custom_call" | custom-call | tf_op jit(solution)/shard_map/pallas_call | solution.py:278
  74.8 0.0 copy-start.2
  74.8 0.8 copy-done.2
  75.6 1.3 %copy.99 = f32[32,30,16]{0,2,1:T(8,128)S(1)} copy(f32[32,30,16]{2,1,0:T(8,128)} %bitcast.25) | data formatting | bytes 122880
  76.9 0.1 copy.92
  77.0 0.1 pad.24.clone
  77.1 11.1 %all_to_all.23 = f32[32,1,483]{2,1,0:T(1,128)S(1)} all-to-all(f32[32,1,483]{2,1,0:T(1,128)S(1)} %all_to_all.16), channel_id=1, replica_groups=mesh['space'=16,'chaos'=32] {'chaos'}, dimensions={0} | all-to-all | bytes 123648 | tf_op jit(solution)/shard_map/all_to_all | solution.py:307
  88.2 0.1 copy.93
  88.4 0.1 slice_reduce_fusion
  88.5 0.6 broadcast_in_dim.76
  89.1 15.3 %all-to-all-start.2 = ((f32[16,1,3]{2,1,0:T(1,128)}), f32[16,1,3]{2,1,0:T(1,128)S(1)}, u32[]{:S(2)}, u32[]{:S(2)}) async-start(f32[16,1,3]{2,1,0:T(1,128)} %broadcast_in_dim.76), calls=%async_computation.2 | async-start | bytes 16384 | tf_op jit(solution)/shard_map/all_to_all | solution.py:312
  104.5 0.2 copy.94
  104.7 0.7 copy.96
  105.4 10.4 %all-to-all-done.2 = f32[16,1,3]{2,1,0:T(1,128)S(1)} async-done(((f32[16,1,3]{2,1,0:T(1,128)}), f32[16,1,3]{2,1,0:T(1,128)S(1)}, u32[]{:S(2)}, u32[]{:S(2)}) %all-to-all-start.2) | async-done | bytes 224 | tf_op jit(solution)/shard_map/all_to_all | solution.py:312
  115.8 0.5 sqrt.3
  (13 shorter events, 0.2 us)
Async XLA Ops:
  2.9 9.2 %collective-permute-start = (f32[43,4,128]{2,1,0:T(4,128)S(1)}, f32[43,4,128]{2,1,0:T(4,128)S(1)}, u32[]{:S(2)}, u32[]{:S(2)}) collective-permute-start(f32[43,4,128]{2,1,0:T(4,128)S(1)} %pad_maximum_fusion.2), channel_id=1, source_target_pairs={{0,32},{32,64},{64,96},{96,128},{128,160},{160,192},{192,224},{224... | collective-permute-start | bytes 264200 | tf_op jit(solution)/shard_map/ppermute | solution.py:215
  7.3 5.4 %collective-permute-start.1 = (f32[43,4,128]{2,1,0:T(4,128)S(1)}, f32[43,4,128]{2,1,0:T(4,128)S(1)}, u32[]{:S(2)}, u32[]{:S(2)}) collective-permute-start(f32[43,4,128]{2,1,0:T(4,128)S(1)} %pad_maximum_fusion.2), channel_id=1, source_target_pairs={{32,0},{64,32},{96,64},{128,96},{160,128},{192,160},{224,192},{256... | collective-permute-start | bytes 264200 | tf_op jit(solution)/shard_map/ppermute | solution.py:216
  15.1 1.6 %copy-start.6 = (f32[43,12,32,12]{0,3,2,1:T(8,128)}, f32[43,12,32,12]{0,3,2,1:T(8,128)S(1)}, u32[]{:S(2)}) copy-start(f32[43,12,32,12]{0,3,2,1:T(8,128)S(1)} %pad_maximum_fusion) | copy-start | bytes 2377732
  19.8 12.2 %copy-start.7 = (s32[32]{0:T(128)S(1)}, s32[32]{0:T(128)}, u32[]{:S(2)}) copy-start(s32[32]{0:T(128)} %param.14) | copy-start | bytes 388
  22.1 25.9 %all-to-all-start = ((f32[32,32,256]{2,1,0:T(8,128)}), f32[32,32,256]{2,1,0:T(8,128)S(1)}, u32[]{:S(2)}, u32[]{:S(2)}) async-start(f32[32,32,256]{2,1,0:T(8,128)} %pad.19.clone), calls=%async_computation | async-start | bytes 2097152 | tf_op jit(solution)/shard_map/all_to_all | solution.py:230
  32.8 15.2 %copy-start = (f32[384,960]{1,0:T(8,128)S(1)}, f32[384,960]{1,0:T(8,128)}, u32[]{:S(2)}) copy-start(f32[384,960]{1,0:T(8,128)} %constant.72.clone.w2_ref) | copy-start | bytes 4423684
  32.8 15.2 %copy-start.3 = (f32[256,128]{1,0:T(8,128)S(1)}, f32[256,128]{1,0:T(8,128)}, u32[]{:S(2)}) copy-start(f32[256,128]{1,0:T(8,128)} %constant.74.clone.picks_ref) | copy-start | bytes 393220
  32.8 15.2 %copy-start.5 = (f32[16,96]{1,0:T(8,128)S(1)}, f32[16,96]{1,0:T(8,128)}, u32[]{:S(2)}) copy-start(f32[16,96]{1,0:T(8,128)} %constant.70.clone.w0_ref) | copy-start | bytes 18436
  48.0 1.4 %copy-start.1 = (f32[80,4416]{1,0:T(8,128)S(1)}, f32[80,4416]{1,0:T(8,128)}, u32[]{:S(2)}) copy-start(f32[80,4416]{1,0:T(8,128)} %constant.73.clone.w3_ref) | copy-start | bytes 4239364
  49.4 0.9 copy-start.4
  74.8 0.8 copy-start.2
  89.1 26.7 %all-to-all-start.2 = ((f32[16,1,3]{2,1,0:T(1,128)}), f32[16,1,3]{2,1,0:T(1,128)S(1)}, u32[]{:S(2)}, u32[]{:S(2)}) async-start(f32[16,1,3]{2,1,0:T(1,128)} %broadcast_in_dim.76), calls=%async_computation.2 | async-start | bytes 16384 | tf_op jit(solution)/shard_map/all_to_all | solution.py:312

commit v2 on v1

--- a/solution.py
+++ b/solution.py
@@ -12,7 +12,8 @@
 M = 12
 P_SIZE = 455
 ITERS = 3
-GHOST = ITERS + 1
+GHOST = ITERS
+MOVED = ITERS + 1
 
 
 spectrum_low = 0.05
@@ -137,11 +138,7 @@
     inside = mask_ref[0:1, :] > 0.5
     own = mask_ref[1:2, :] > 0.5
     weights = [[0.5 * (fields[k : k + 1] + near(fields, s)[k : k + 1]) for s in shifts] for k in range(M + 1)]
-    mean_now = fields[0:1]
-    diagonal = 0.5 * (mean_now + near(mean_now, shifts[0]))
-    for s in shifts[1:]:
-        diagonal = diagonal + 0.5 * (mean_now + near(mean_now, s))
-    diagonal = jnp.where(inside, diagonal, 1.0)
+    diagonal = jnp.where(inside, mask_ref[2:3, :], 1.0)
     stacks = (s0_ref, s1_ref, s2_ref, s3_ref)
     mats = (w0_ref, w1_ref, w2_ref, w3_ref)
 
@@ -202,8 +199,8 @@
     my_row_block = lax.axis_index("space")
     my_col_block = lax.axis_index("chaos")
     width = cols // n_chaos
-    ghost = GHOST
-    assert rows >= ghost and ghost % width == 0 and width * n_chaos == cols
+    ghost, moved = GHOST, MOVED
+    assert rows >= moved and moved % width == 0 and width * n_chaos == cols
     patch_rows, patch_cols = rows + 2 * ghost, width + 2 * ghost
     cells = patch_rows * patch_cols
     count = P_SIZE
@@ -212,16 +209,19 @@
     block = jnp.concatenate([forcing, fields], axis=0)
     down_pairs = [(i, i + 1) for i in range(n_space - 1)]
     up_pairs = [(i + 1, i) for i in range(n_space - 1)]
-    above = lax.ppermute(block[:, rows - ghost :], "space", down_pairs)
-    below = lax.ppermute(block[:, :ghost], "space", up_pairs)
+    above = lax.ppermute(block[:, rows - moved :], "space", down_pairs)
+    below = lax.ppermute(block[:, :moved], "space", up_pairs)
     tall = jnp.concatenate([above, block, below], axis=1)
-    tall = jnp.pad(tall, ((0, 0), (0, 0), (ghost, ghost)))
-
-    side = ghost // width
-    pieces = tall.reshape(tall.shape[0], patch_rows, n_chaos + 2 * side, width)
-    windows = jnp.concatenate(
+    tall = jnp.pad(tall, ((0, 0), (0, 0), (moved, moved)))
+
+    side = moved // width
+    wide_rows = rows + 2 * moved
+    pieces = tall.reshape(tall.shape[0], wide_rows, n_chaos + 2 * side, width)
+    wide = jnp.concatenate(
         [pieces[:, :, j : j + n_chaos] for j in range(2 * side + 1)], axis=-1
     )
+    trim = moved - ghost
+    windows = wide[:, trim : wide_rows - trim, :, trim : width + 2 * moved - trim]
     lanes = -(-cells // 128) * 128
     assert cells + patch_cols <= lanes
     slot_rows = -(-(cap + 1) // 8) * 8
@@ -231,6 +231,14 @@
     by_slot = got.reshape(n_chaos * slot_rows, lanes)
     my_fields = lax.dynamic_index_in_dim(windows[cap:], my_col_block, axis=2, keepdims=False)
     my_fields = my_fields.reshape(M + 1, cells)
+    mean_wide = lax.dynamic_index_in_dim(wide[cap], my_col_block, axis=1, keepdims=False)
+    mean_pad = jnp.pad(mean_wide, 1)
+    centre = mean_pad[1:-1, 1:-1]
+    diagonal = 0.5 * (centre + mean_pad[:-2, 1:-1])
+    diagonal = diagonal + 0.5 * (centre + mean_pad[2:, 1:-1])
+    diagonal = diagonal + 0.5 * (centre + mean_pad[1:-1, 2:])
+    diagonal = diagonal + 0.5 * (centre + mean_pad[1:-1, :-2])
+    diagonal = diagonal[trim : trim + patch_rows, trim : trim + patch_cols].reshape(cells)
 
     blocks, row_of, total = coupling_blocks(M)
     sizes, firsts, padded, offsets = degree_layout(M)
@@ -268,8 +276,8 @@
 
     field_rows = -(-(M + 1) // 8) * 8
     field_in = jnp.pad(my_fields, ((0, field_rows - (M + 1)), (0, lanes - cells)))
-    masks = jnp.stack([inside, own]).astype(jnp.float32)
-    masks = jnp.pad(masks, ((0, 6), (0, lanes - cells)))
+    masks = jnp.stack([inside.astype(jnp.float32), own.astype(jnp.float32), diagonal])
+    masks = jnp.pad(masks, ((0, 5), (0, lanes - cells)))
     mats = [jnp.asarray(blocks[d]) for d in range(4)]
     own_lanes = np.flatnonzero(np.pad(np.ones((rows, width)), ghost).reshape(-1) > 0.5)
     picks = np.zeros((lanes, 128), np.float32)

time: 117 us -> 104 us (0.89)
  Pallas kernels: 24.5 us -> 17.5 us
  waiting for transfers between devices: 18.8 us -> 15.2 us
  local copies, waits for them, and re-layouts: 24.7 us -> 21.3 us
    pallas_call x1, Pallas kernels: 24.5 us -> 17.5 us  [local(): pl.pallas_call(functools.partial(sweeps, padded=tuple((int(v) for v in pa...]
    unnamed x21 -> x19, local copies, waits for them, and re-layouts: 9.81 us -> 5.87 us
    reshape x2, local copies, waits for them, and re-layouts: 3.1 us -> 0.08 us  [local(): my_fields = my_fields.reshape(M + 1, cells)]
    all_to_all x1, waiting for transfers between devices: 7.84 us -> 4.95 us  [local(): got = lax.all_to_all(sent, 'chaos', 0, 0, tiled=True)]
    slice x0 -> x2, local copies, waits for them, and re-layouts: none -> 2.72 us  [the longest x1 2.65 us: local(): wide[cap]]
    all_to_all x1, starting transfers between devices: 15.3 us -> 16.9 us  [local(): all_rows = lax.all_to_all(spread, 'space', 0, 0, tiled=True)]
    pad x1, local copies, waits for them, and re-layouts: 2.34 us -> 0.85 us  [local(): sent = jnp.pad(sent, ((0, 0), (0, slot_rows - cap), (0, lanes - cells)))]
  transfers between devices with their start and end apart: 4 -> 4, of which waited for: 3 -> 2; matrix products, arithmetic and copies ran while one was open for 11% -> 13% of each run, Pallas kernels for 0% -> 0%
where the time goes in v2:
time: 104 us; the launch traced here: 103 us
  starting transfers between devices  30.7 us (30%)
  local copies, waits for them, and re-layouts  21.3 us (20%)
  Pallas kernels  17.5 us (17%)
  waiting for transfers between devices  15.2 us (15%)
  blocking collectives  10.8 us (10%)
  other arithmetic  6.96 us (7%)
    pallas_call x1, Pallas kernels, local(): pl.pallas_call(functools.partial(sweeps, padded=tuple((int(v) for v in pa...  17.5 us
    all_to_all x1, starting transfers between devices, local(): all_rows = lax.all_to_all(spread, 'space', 0, 0, tiled=True)  16.9 us
    all_to_all x1, blocking collectives, local(): back = lax.all_to_all(payload, 'chaos', 0, 0, tiled=True)  10.8 us
    all_to_all x1, waiting for transfers between devices, local(): all_rows = lax.all_to_all(spread, 'space', 0, 0, tiled=True)  10.3 us
    all_to_all x1, starting transfers between devices, local(): got = lax.all_to_all(sent, 'chaos', 0, 0, tiled=True)  8.22 us
    unnamed x19, local copies, waits for them, and re-layouts  5.87 us
    all_to_all x1, waiting for transfers between devices, local(): got = lax.all_to_all(sent, 'chaos', 0, 0, tiled=True)  4.95 us
    ppermute x1, starting transfers between devices, local(): above = lax.ppermute(block[:, rows - moved:], 'space', down_pairs)  4.36 us
  transfers between devices with their start and end apart: 4, of which 2 were waited for; matrix products, arithmetic and copies ran while one was open for 13% of the time, Pallas kernels for 0%

profile of v2, /device:TPU:1, one launch (start us, length us, event | category | flops | bytes accessed | tf_op | source)
XLA Modules:
  0.0 103.4 jit_solution(15271203034803776066)
XLA Ops:
  0.6 0.7 broadcast.178
  1.3 0.7 broadcast_multiply_fusion
  2.1 0.9 pad_maximum_fusion.2
  2.9 4.4 %collective-permute-start = (f32[43,4,128]{2,1,0:T(4,128)S(1)}, f32[43,4,128]{2,1,0:T(4,128)S(1)}, u32[]{:S(2)}, u32[]{:S(2)}) collective-permute-start(f32[43,4,128]{2,1,0:T(4,128)S(1)} %pad_maximum_fusion.2), channel_id=1, source_target_pairs={{0,32},{32,64},{64,96},{96,128},{128,160},{160,192},{192,224},{224... | collective-permute-start | bytes 264200 | tf_op jit(solution)/shard_map/ppermute | solution.py:212
  7.3 1.3 %collective-permute-start.1 = (f32[43,4,128]{2,1,0:T(4,128)S(1)}, f32[43,4,128]{2,1,0:T(4,128)S(1)}, u32[]{:S(2)}, u32[]{:S(2)}) collective-permute-start(f32[43,4,128]{2,1,0:T(4,128)S(1)} %pad_maximum_fusion.2), channel_id=1, source_target_pairs={{32,0},{64,32},{96,64},{128,96},{160,128},{192,160},{224,192},{256... | collective-permute-start | bytes 264200 | tf_op jit(solution)/shard_map/ppermute | solution.py:213
  8.6 0.1 and_convert_fusion
  8.7 0.7 iota_compare_fusion
  9.4 0.7 copy.97
  10.2 0.1 reduce-window.8
  10.2 0.1 reduce.1
  10.3 0.7 fusion.5
  11.0 0.1 iota_add_fusion
  11.1 0.5 add.114
  11.6 0.6 lt.66
  12.2 0.1 and_convert_fusion.1
  12.3 0.8 select_reduce_fusion
  13.1 0.2 add_select_fusion.row_of_slot_ref
  13.2 0.7 add_select_fusion.1
  14.0 0.1 reshape.226
  14.0 0.1 reshape.227
  14.1 0.1 copy.104.slot_of_row_ref
  14.3 0.0 collective-permute-done
  14.3 0.0 collective-permute-done.1
  14.3 0.9 pad_maximum_fusion.1
  15.2 0.3 copy.114
  15.5 0.1 pad.20.clone
  15.6 0.3 fusion.4
  15.9 0.7 pad_maximum_fusion
  16.7 2.6 %slice.73 = f32[1,12,32,12]{0,3,2,1:T(8,128)} slice(f32[43,12,32,12]{0,3,2,1:T(8,128)S(1)} %pad_maximum_fusion), slice={[30:31], [0:12], [0:32], [0:12]} | slice | bytes 36864 | tf_op jit(solution)/shard_map/slice | solution.py:234
  19.3 0.2 slice_bitcast_fusion
  19.6 0.5 copy.95
  20.1 1.2 %copy.115 = f32[32,30,100]{2,1,0:T(8,128)S(1)} copy(f32[32,30,100]{1,0,2:T(8,128)S(1)} %bitcast.27) | data formatting | bytes 768000
  21.2 0.9 pad.21.clone
  22.1 8.2 %all-to-all-start = ((f32[32,32,128]{2,1,0:T(8,128)}), f32[32,32,128]{2,1,0:T(8,128)S(1)}, u32[]{:S(2)}, u32[]{:S(2)}) async-start(f32[32,32,128]{2,1,0:T(8,128)} %pad.21.clone), calls=%async_computation | async-start | bytes 1048576 | tf_op jit(solution)/shard_map/all_to_all | solution.py:230
  30.3 0.0 copy-start
  30.3 0.0 copy-start.2
  30.3 0.0 copy-start.3
  30.4 1.1 %dynamic-slice_reduce_fusion = f32[12,12]{1,0:T(8,128)S(1)} fusion(f32[1,12,32,12]{0,3,2,1:T(8,128)} %slice.73, s32[]{:T(128)S(6)} %select_n.62), kind=kLoop, calls=%fused_computation.4 | loop fusion | bytes 1156 | tf_op jit(solution)/shard_map/jit(dynamic_index_in_dim)/dynamic_slice | solution.py:234
  31.5 0.1 pad_slice_fusion.3
  31.6 4.0 %slice.72 = f32[13,10,32,10]{0,3,2,1:T(8,128)} slice(f32[43,12,32,12]{0,3,2,1:T(8,128)} %copy-done.6), slice={[30:43], [1:11], [0:32], [1:11]} | slice | bytes 332800 | tf_op jit(solution)/shard_map/slice | solution.py:232
  35.6 0.1 fusion.1
  35.7 0.1 stack_reshape.3
  35.8 0.9 constant_dynamic-slice_fusion
  36.7 0.1 copy.111
  36.8 5.0 %all-to-all-done = f32[32,32,128]{2,1,0:T(8,128)S(1)} async-done(((f32[32,32,128]{2,1,0:T(8,128)}), f32[32,32,128]{2,1,0:T(8,128)S(1)}, u32[]{:S(2)}, u32[]{:S(2)}) %all-to-all-start) | async-done | bytes 524320 | tf_op jit(solution)/shard_map/all_to_all | solution.py:230
  41.7 0.0 copy-start.1
  41.8 1.4 %copy-done.1 = f32[80,4416]{1,0:T(8,128)S(1)} copy-done((f32[80,4416]{1,0:T(8,128)S(1)}, f32[80,4416]{1,0:T(8,128)}, u32[]{:S(2)}) %copy-start.1) | copy-done | bytes 1413144
  43.1 0.7 copy-done.4
  43.8 17.5 %shard_map.122 = (f32[1024,128]{1,0:T(8,128)S(1)}, f32[8,128]{1,0:T(8,128)S(1)}) custom-call(f32[1024,128]{1,0:T(8,128)S(1)} %bitcast.24, s32[472,1]{1,0:T(8,128)S(1)} %copy.104.slot_of_row_ref, s32[1024,1]{1,0:T(8,128)S(1)} %add_select_fusion.row_of_slot_ref, f32[128,128]{1,0:T(8,128)S(1)} %copy-done.3, f32[16,128]{1,0:T(8,128)S(1)} %pad.22.field_ref, ...), custom_call_target="tpu_custom_call" | custom-call | tf_op jit(solution)/shard_map/pallas_call | solution.py:286
  61.3 0.0 copy-start.5
  61.3 0.6 copy-done.5
  61.9 0.3 copy.113
  62.2 0.1 copy.106
  62.3 0.7 slice_bitcast_fusion.1
  63.0 0.1 pad.26.clone
  63.1 10.8 %all_to_all.23 = f32[32,1,483]{2,1,0:T(1,128)S(1)} all-to-all(f32[32,1,483]{2,1,0:T(1,128)S(1)} %all_to_all.16), channel_id=1, replica_groups=mesh['space'=16,'chaos'=32] {'chaos'}, dimensions={0} | all-to-all | bytes 123648 | tf_op jit(solution)/shard_map/all_to_all | solution.py:315
  73.9 0.1 copy.107
  74.0 0.1 slice_reduce_fusion
  74.1 0.6 broadcast_in_dim.76
  74.7 16.9 %all-to-all-start.2 = ((f32[16,1,3]{2,1,0:T(1,128)}), f32[16,1,3]{2,1,0:T(1,128)S(1)}, u32[]{:S(2)}, u32[]{:S(2)}) async-start(f32[16,1,3]{2,1,0:T(1,128)} %broadcast_in_dim.76), calls=%async_computation.2 | async-start | bytes 16384 | tf_op jit(solution)/shard_map/all_to_all | solution.py:320
  91.6 0.2 copy.108
  91.8 0.7 copy.110
  92.6 10.3 %all-to-all-done.2 = f32[16,1,3]{2,1,0:T(1,128)S(1)} async-done(((f32[16,1,3]{2,1,0:T(1,128)}), f32[16,1,3]{2,1,0:T(1,128)S(1)}, u32[]{:S(2)}, u32[]{:S(2)}) %all-to-all-start.2) | async-done | bytes 224 | tf_op jit(solution)/shard_map/all_to_all | solution.py:320
  102.9 0.5 sqrt.3
  (15 shorter events, 0.2 us)
Async XLA Ops:
  2.9 11.3 %collective-permute-start = (f32[43,4,128]{2,1,0:T(4,128)S(1)}, f32[43,4,128]{2,1,0:T(4,128)S(1)}, u32[]{:S(2)}, u32[]{:S(2)}) collective-permute-start(f32[43,4,128]{2,1,0:T(4,128)S(1)} %pad_maximum_fusion.2), channel_id=1, source_target_pairs={{0,32},{32,64},{64,96},{96,128},{128,160},{160,192},{192,224},{224... | collective-permute-start | bytes 264200 | tf_op jit(solution)/shard_map/ppermute | solution.py:212
  7.3 7.0 %collective-permute-start.1 = (f32[43,4,128]{2,1,0:T(4,128)S(1)}, f32[43,4,128]{2,1,0:T(4,128)S(1)}, u32[]{:S(2)}, u32[]{:S(2)}) collective-permute-start(f32[43,4,128]{2,1,0:T(4,128)S(1)} %pad_maximum_fusion.2), channel_id=1, source_target_pairs={{32,0},{64,32},{96,64},{128,96},{160,128},{192,160},{224,192},{256... | collective-permute-start | bytes 264200 | tf_op jit(solution)/shard_map/ppermute | solution.py:213
  16.7 2.7 %copy-start.6 = (f32[43,12,32,12]{0,3,2,1:T(8,128)}, f32[43,12,32,12]{0,3,2,1:T(8,128)S(1)}, u32[]{:S(2)}) copy-start(f32[43,12,32,12]{0,3,2,1:T(8,128)S(1)} %pad_maximum_fusion) | copy-start | bytes 2377732
  22.1 19.6 %all-to-all-start = ((f32[32,32,128]{2,1,0:T(8,128)}), f32[32,32,128]{2,1,0:T(8,128)S(1)}, u32[]{:S(2)}, u32[]{:S(2)}) async-start(f32[32,32,128]{2,1,0:T(8,128)} %pad.21.clone), calls=%async_computation | async-start | bytes 1048576 | tf_op jit(solution)/shard_map/all_to_all | solution.py:230
  30.3 11.4 %copy-start = (f32[384,960]{1,0:T(8,128)S(1)}, f32[384,960]{1,0:T(8,128)}, u32[]{:S(2)}) copy-start(f32[384,960]{1,0:T(8,128)} %constant.78.clone.w2_ref) | copy-start | bytes 4423684
  30.3 11.4 %copy-start.2 = (f32[88,192]{1,0:T(8,128)S(1)}, f32[88,192]{1,0:T(8,128)}, u32[]{:S(2)}) copy-start(f32[88,192]{1,0:T(8,128)} %constant.77.clone.w1_ref) | copy-start | bytes 202756
  30.3 11.4 %copy-start.3 = (f32[128,128]{1,0:T(8,128)S(1)}, f32[128,128]{1,0:T(8,128)}, u32[]{:S(2)}) copy-start(f32[128,128]{1,0:T(8,128)} %constant.80.clone.picks_ref) | copy-start | bytes 196612
  41.7 1.4 %copy-start.1 = (f32[80,4416]{1,0:T(8,128)S(1)}, f32[80,4416]{1,0:T(8,128)}, u32[]{:S(2)}) copy-start(f32[80,4416]{1,0:T(8,128)} %constant.79.clone.w3_ref) | copy-start | bytes 4239364
  43.1 0.7 copy-start.4
  61.3 0.6 copy-start.5
  74.7 28.1 %all-to-all-start.2 = ((f32[16,1,3]{2,1,0:T(1,128)}), f32[16,1,3]{2,1,0:T(1,128)S(1)}, u32[]{:S(2)}, u32[]{:S(2)}) async-start(f32[16,1,3]{2,1,0:T(1,128)} %broadcast_in_dim.76), calls=%async_computation.2 | async-start | bytes 16384 | tf_op jit(solution)/shard_map/all_to_all | solution.py:320

commit v3 on v2

--- a/solution.py
+++ b/solution.py
@@ -278,7 +278,18 @@
     field_in = jnp.pad(my_fields, ((0, field_rows - (M + 1)), (0, lanes - cells)))
     masks = jnp.stack([inside.astype(jnp.float32), own.astype(jnp.float32), diagonal])
     masks = jnp.pad(masks, ((0, 5), (0, lanes - cells)))
-    mats = [jnp.asarray(blocks[d]) for d in range(4)]
+    mats = []
+    for d in range(4):
+        height, wide_cols = blocks[d].shape
+        part = blocks[d].reshape(height, M, wide_cols // M)
+        assert np.all((part != 0).sum(axis=2) <= 1)
+        partner = np.where(part.any(axis=2), part.argmax(axis=2), -1).astype(np.int32)
+        value = part.max(axis=2).astype(np.float32)
+        place = lax.broadcasted_iota(jnp.int32, part.shape, 2)
+        built = jnp.where(
+            place == jnp.asarray(partner)[:, :, None], jnp.asarray(value)[:, :, None], 0.0
+        )
+        mats.append(built.reshape(height, wide_cols))
     own_lanes = np.flatnonzero(np.pad(np.ones((rows, width)), ghost).reshape(-1) > 0.5)
     picks = np.zeros((lanes, 128), np.float32)
     picks[own_lanes, np.arange(own_lanes.size)] = 1.0

time: 104 us -> 143 us (1.38)
  local copies, waits for them, and re-layouts: 21.3 us -> 52.9 us
  other arithmetic: 6.96 us -> 13.7 us
  waiting for transfers between devices: 15.2 us -> 10.4 us
  blocking collectives: 10.8 us -> 14.5 us
    unnamed x19 -> x57, local copies, waits for them, and re-layouts: 5.87 us -> 13.4 us
    eq x0 -> x8, local copies, waits for them, and re-layouts: none -> 6.64 us  [local(): place == jnp.asarray(partner)[:, :, None]]
    all_to_all x1, waiting for transfers between devices: 4.95 us -> 0.01 us  [local(): got = lax.all_to_all(sent, 'chaos', 0, 0, tiled=True)]
    broadcast_in_dim x0 -> x8, local copies, waits for them, and re-layouts: none -> 4.86 us  [local(): jnp.where(place == jnp.asarray(partner)[:, :, None], jnp.asarray(value)[:...]
    all_to_all x1, blocking collectives: 10.8 us -> 14.5 us  [local(): back = lax.all_to_all(payload, 'chaos', 0, 0, tiled=True)]
    reshape x2, local copies, waits for them, and re-layouts: 0.08 us -> 2.99 us  [local(): my_fields = my_fields.reshape(M + 1, cells)]
    select_n x0 -> x4, other arithmetic: none -> 2.62 us  [local(): jnp.where(place == jnp.asarray(partner)[:, :, None], jnp.asarray(value)[:...]
    iota x0 -> x8, local copies, waits for them, and re-layouts: none -> 2.01 us  [local(): place = lax.broadcasted_iota(jnp.int32, part.shape, 2)]
  transfers between devices with their start and end apart: 4 -> 4, of which waited for: 2 -> 1; matrix products, arithmetic and copies ran while one was open for 13% -> 28% of each run, Pallas kernels for 0% -> 0%
where the time goes in v3:
time: 143 us; the launch traced here: 142 us
  local copies, waits for them, and re-layouts  52.9 us (37%)
  starting transfers between devices  30.8 us (22%)
  Pallas kernels  18.5 us (13%)
  blocking collectives  14.5 us (10%)
  other arithmetic  13.7 us (10%)
  waiting for transfers between devices  10.4 us (7%)
    pallas_call x1, Pallas kernels, local(): pl.pallas_call(functools.partial(sweeps, padded=tuple((int(v) for v in pa...  18.5 us
    all_to_all x1, starting transfers between devices, local(): all_rows = lax.all_to_all(spread, 'space', 0, 0, tiled=True)  16.2 us
    all_to_all x1, blocking collectives, local(): back = lax.all_to_all(payload, 'chaos', 0, 0, tiled=True)  14.5 us
    unnamed x57, local copies, waits for them, and re-layouts  13.4 us
    all_to_all x1, waiting for transfers between devices, local(): all_rows = lax.all_to_all(spread, 'space', 0, 0, tiled=True)  10.4 us
    all_to_all x1, starting transfers between devices, local(): got = lax.all_to_all(sent, 'chaos', 0, 0, tiled=True)  8.27 us
    eq x8, local copies, waits for them, and re-layouts, local(): place == jnp.asarray(partner)[:, :, None]  6.64 us
    ppermute x1, starting transfers between devices, local(): above = lax.ppermute(block[:, rows - moved:], 'space', down_pairs)  4.99 us
  transfers between devices with their start and end apart: 4, of which 1 were waited for; matrix products, arithmetic and copies ran while one was open for 28% of the time, Pallas kernels for 0%

profile of v3, /device:TPU:1, one launch (start us, length us, event | category | flops | bytes accessed | tf_op | source)
XLA Modules:
  0.0 141.8 jit_solution(1494527051211220702)
XLA Ops:
  0.6 0.7 broadcast.210
  1.3 0.7 broadcast_multiply_fusion
  2.1 0.6 copy-done.9
  2.7 1.5 %pad_maximum_fusion.2 = f32[43,4,128]{2,1,0:T(4,128)} fusion(f32[12,4,128]{2,1,0:T(4,128)S(1)} %bitcast.44, f32[1,4,128]{2,1,0:T(4,128)} %bitcast.47, f32[30,4,128]{2,1,0:T(4,128)} %param.15), kind=kLoop, calls=%fused_computation.8 | loop fusion | flops 44032 | bytes 176128 | tf_op jit(solution)/shard_map/concatenate | solution.py:209
  4.2 5.0 %collective-permute-start = (f32[43,4,128]{2,1,0:T(4,128)}, f32[43,4,128]{2,1,0:T(4,128)}, u32[]{:S(2)}, u32[]{:S(2)}) collective-permute-start(f32[43,4,128]{2,1,0:T(4,128)} %pad_maximum_fusion.2), channel_id=1, source_target_pairs={{0,32},{32,64},{64,96},{96,128},{128,160},{160,192},{192,224},{224... | collective-permute-start | bytes 264200 | tf_op jit(solution)/shard_map/ppermute | solution.py:212
  9.2 1.3 collective-permute-start.1
  10.5 0.7 and_convert_fusion
  11.1 0.7 iota_compare_fusion
  11.9 0.7 copy.131
  12.8 1.2 fusion.5
  14.0 1.3 add.114
  15.4 0.6 lt.66
  15.9 1.0 broadcast_in_dim.147
  17.0 0.7 broadcast_in_dim.148
  17.7 1.0 eq.53
  18.7 1.8 %eq.54 = s32[80,4416]{1,0:T(8,128)} reshape(s32[80,12,368]{2,1,0:T(8,128)S(1)} %eq.53) | data formatting | bytes 2826240 | tf_op jit(solution)/shard_map/eq | solution.py:290
  20.6 0.8 eq.50
  21.4 1.6 %copy.142 = s32[384,960]{1,0:T(8,128)} copy(s32[384,960]{0,1:T(8,128)S(1)} %bitcast.35) | data formatting | bytes 2949120 | tf_op jit(solution)/shard_map/eq | solution.py:290
  23.2 1.7 %copy.143 = f32[384,960]{1,0:T(8,128)} copy(f32[384,960]{0,1:T(8,128)S(1)} %bitcast.36) | data formatting | bytes 2949120 | tf_op jit(solution)/shard_map/jit(_where)/broadcast_in_dim | solution.py:289
  24.9 0.7 iota.77
  25.5 0.7 copy.140
  26.3 0.7 copy.141
  27.0 0.6 iota.74
  27.7 0.6 copy.138
  28.3 0.7 copy.139
  29.0 0.6 iota.71
  29.6 0.7 and_convert_fusion.1
  30.4 1.2 add_select_fusion.row_of_slot_ref
  31.6 1.7 %compare_select_fusion.1.w3_ref = f32[80,4416]{1,0:T(8,128)S(1)} fusion(f32[80,4416]{1,0:T(8,128)S(1)} %broadcast_in_dim.148, s32[80,4416]{1,0:T(8,128)} %eq.54, s32[4416]{0:T(1024)S(1)} %iota.80), kind=kLoop, calls=%fused_computation.3 | loop fusion | flops 706560 | bytes 4257024 | tf_op jit(solution)/shard_map/jit(_where)/select_n | solution.py:289
  34.3 0.5 copy-done.7
  34.9 0.7 compare_select_fusion.2.w1_ref
  35.5 0.6 add_select_fusion.1
  36.1 0.6 reshape.250
  36.8 0.6 reshape.251
  37.3 1.5 %copy.144.slot_of_row_ref = s32[472,1]{1,0:T(8,128)} copy(s32[472,1]{0,1:T(1,128)} %bitcast.50) | data formatting | bytes 3776 | tf_op jit(solution)/shard_map/broadcast_in_dim | solution.py:313
  38.9 1.8 %pad_maximum_fusion.1 = f32[43,12,128]{2,1,0:T(8,128)} fusion(f32[43,4,128]{2,1,0:T(4,128)} %collective-permute-done.1, f32[12,4,128]{2,1,0:T(4,128)} %bitcast.45, f32[1,4,128]{2,1,0:T(4,128)} %bitcast.48, f32[30,4,128]{2,1,0:T(4,128)} %param.15, f32[43,4,128]{2,1,0:T(4,128)} %collective-permute-done), kind=kLoop, calls=%fused_computation.5 | loop fusion | flops 264192 | bytes 528384 | tf_op jit(solution)/shard_map/concatenate | solution.py:214
  40.7 2.2 %copy.154 = f32[43,12,128]{0,2,1:T(8,128)} copy(f32[43,12,128]{2,1,0:T(8,128)} %pad_maximum_fusion.1) | data formatting | bytes 528384
  42.8 1.2 pad.20.clone
  44.4 0.7 pad_maximum_fusion
  45.1 2.7 %slice.73 = f32[1,12,32,12]{0,3,2,1:T(8,128)} slice(f32[43,12,32,12]{0,3,2,1:T(8,128)S(1)} %pad_maximum_fusion), slice={[30:31], [0:12], [0:32], [0:12]} | slice | bytes 36864 | tf_op jit(solution)/shard_map/slice | solution.py:234
  48.0 1.7 %copy.129 = f32[32,30,10,10]{1,0,3,2:T(8,128)} copy(f32[32,30,10,10]{1,3,0,2:T(8,128)S(1)} %slice_bitcast_fusion) | data formatting | bytes 768000 | tf_op jit(solution)/shard_map/transpose | solution.py:228
  49.7 3.2 %copy.155 = f32[32,30,100]{2,1,0:T(8,128)} copy(f32[32,30,100]{1,0,2:T(8,128)} %bitcast.34) | data formatting | bytes 768000
  52.9 1.9 %pad.21.clone = f32[32,32,128]{2,1,0:T(8,128)} pad(f32[32,30,100]{2,1,0:T(8,128)} %copy.155, f32[]{:T(128)} %constant.30.clone.1), padding=0_0x0_2x0_28 | pad | bytes 908292 | tf_op jit(solution)/shard_map/jit(_pad)/pad | solution.py:229
  54.8 8.3 %all-to-all-start = ((f32[32,32,128]{2,1,0:T(8,128)}), f32[32,32,128]{2,1,0:T(8,128)}, u32[]{:S(2)}, u32[]{:S(2)}) async-start(f32[32,32,128]{2,1,0:T(8,128)} %pad.21.clone), calls=%async_computation | async-start | bytes 1048576 | tf_op jit(solution)/shard_map/all_to_all | solution.py:230
  63.0 1.0 dynamic-slice_reduce_fusion
  64.1 4.0 %slice.72 = f32[13,10,32,10]{0,3,2,1:T(8,128)} slice(f32[43,12,32,12]{0,3,2,1:T(8,128)} %copy-done.4), slice={[30:43], [1:11], [0:32], [1:11]} | slice | bytes 332800 | tf_op jit(solution)/shard_map/slice | solution.py:232
  68.2 0.6 stack_reshape.3
  68.8 1.5 %constant_dynamic-slice_fusion = f32[13,10,1,10]{0,3,2,1:T(8,128)} fusion(f32[13,10,32,10]{0,3,2,1:T(8,128)} %slice.72, s32[]{:T(128)S(6)} %select_n.82), kind=kLoop, calls=%fused_computation.41 | loop fusion | bytes 10404 | tf_op jit(solution)/shard_map/jit(dynamic_index_in_dim)/dynamic_slice | solution.py:232
  70.3 1.5 %reshape.252 = f32[13,100]{0,1:T(8,128)} reshape(f32[13,10,1,10]{0,3,2,1:T(8,128)} %constant_dynamic-slice_fusion) | data formatting | bytes 10400 | tf_op jit(solution)/shard_map/reshape | solution.py:233
  71.9 1.5 %copy.151 = f32[13,100]{1,0:T(8,128)} copy(f32[13,100]{0,1:T(8,128)} %reshape.252) | data formatting | bytes 10400 | tf_op jit(solution)/shard_map/reshape | solution.py:233
  73.3 0.7 pad.22.field_ref
  74.0 0.7 select_maximum_fusion.mask_ref
  74.7 0.9 copy-done
  75.7 0.9 copy-done.2
  76.6 0.8 copy-done.3
  77.4 18.5 %shard_map.158 = (f32[1024,128]{1,0:T(8,128)S(1)}, f32[8,128]{1,0:T(8,128)S(1)}) custom-call(f32[1024,128]{1,0:T(8,128)} %bitcast.4.slots_ref, s32[472,1]{1,0:T(8,128)S(1)} %copy-done, s32[1024,1]{1,0:T(8,128)S(1)} %add_select_fusion.row_of_slot_ref, f32[128,128]{1,0:T(8,128)S(1)} %copy-done.3, f32[16,128]{1,0:T(8,128)S(1)} %pad.22.field_ref, ...), custom_call_target="tpu_custom_call" | custom-call | tf_op jit(solution)/shard_map/pallas_call | solution.py:297
  95.9 0.8 copy-done.1
  96.7 1.3 copy.153
  98.3 14.5 %all_to_all.23 = f32[32,1,483]{2,1,0:T(1,128)S(1)} all-to-all(f32[32,1,483]{2,1,0:T(1,128)S(1)} %all_to_all.16), channel_id=1, replica_groups=mesh['space'=16,'chaos'=32] {'chaos'}, dimensions={0} | all-to-all | bytes 123648 | tf_op jit(solution)/shard_map/all_to_all | solution.py:326
  113.0 0.6 broadcast_in_dim.152
  113.7 16.2 %all-to-all-start.2 = ((f32[16,1,3]{2,1,0:T(1,128)}), f32[16,1,3]{2,1,0:T(1,128)S(1)}, u32[]{:S(2)}, u32[]{:S(2)}) async-start(f32[16,1,3]{2,1,0:T(1,128)} %broadcast_in_dim.152), calls=%async_computation.2 | async-start | bytes 16384 | tf_op jit(solution)/shard_map/all_to_all | solution.py:331
  130.1 0.7 copy.150
  130.9 10.4 %all-to-all-done.2 = f32[16,1,3]{2,1,0:T(1,128)S(1)} async-done(((f32[16,1,3]{2,1,0:T(1,128)}), f32[16,1,3]{2,1,0:T(1,128)S(1)}, u32[]{:S(2)}, u32[]{:S(2)}) %all-to-all-start.2) | async-done | bytes 224 | tf_op jit(solution)/shard_map/all_to_all | solution.py:331
  141.3 0.5 sqrt.3
  (81 shorter events, 3.1 us)
Async XLA Ops:
  2.1 0.6 copy-start.9
  4.2 34.7 %collective-permute-start = (f32[43,4,128]{2,1,0:T(4,128)}, f32[43,4,128]{2,1,0:T(4,128)}, u32[]{:S(2)}, u32[]{:S(2)}) collective-permute-start(f32[43,4,128]{2,1,0:T(4,128)} %pad_maximum_fusion.2), channel_id=1, source_target_pairs={{0,32},{32,64},{64,96},{96,128},{128,160},{160,192},{192,224},{224... | collective-permute-start | bytes 264200 | tf_op jit(solution)/shard_map/ppermute | solution.py:212
  9.2 29.7 %collective-permute-start.1 = (f32[43,4,128]{2,1,0:T(4,128)}, f32[43,4,128]{2,1,0:T(4,128)}, u32[]{:S(2)}, u32[]{:S(2)}) collective-permute-start(f32[43,4,128]{2,1,0:T(4,128)} %pad_maximum_fusion.2), channel_id=1, source_target_pairs={{32,0},{64,32},{96,64},{128,96},{160,128},{192,160},{224,192},{256... | collective-permute-start | bytes 264200 | tf_op jit(solution)/shard_map/ppermute | solution.py:213
  21.4 1.6 %copy-start.14 = (f32[384,12]{0,1:T(8,128)S(1)}, f32[384,12]{0,1:T(8,128)}, u32[]{:S(2)}) copy-start(f32[384,12]{0,1:T(8,128)} %constant.89.clone) | copy-start | bytes 55300
  23.1 2.4 %copy-start.21 = (s32[88,12]{0,1:T(8,128)S(1)}, s32[88,12]{0,1:T(8,128)}, u32[]{:S(2)}) copy-start(s32[88,12]{0,1:T(8,128)} %constant.86.clone) | copy-start | bytes 12676
  23.1 3.2 %copy-start.20 = (f32[88,12]{0,1:T(8,128)S(1)}, f32[88,12]{0,1:T(8,128)}, u32[]{:S(2)}) copy-start(f32[88,12]{0,1:T(8,128)} %constant.87.clone) | copy-start | bytes 12676
  23.2 4.5 %copy-start.17 = (s32[16,12]{0,1:T(8,128)S(1)}, s32[16,12]{0,1:T(8,128)}, u32[]{:S(2)}) copy-start(s32[16,12]{0,1:T(8,128)} %constant.84.clone) | copy-start | bytes 2308
  23.2 5.1 %copy-start.16 = (f32[16,12]{0,1:T(8,128)S(1)}, f32[16,12]{0,1:T(8,128)}, u32[]{:S(2)}) copy-start(f32[16,12]{0,1:T(8,128)} %constant.85.clone) | copy-start | bytes 2308
  23.2 7.1 %copy-start.18 = (s32[472]{0:T(512)S(1)}, s32[472]{0:T(512)}, u32[]{:S(2)}) copy-start(s32[472]{0:T(512)} %constant.82.clone) | copy-start | bytes 5668
  23.2 7.1 %copy-start.24 = (s32[32]{0:T(128)S(1)}, s32[32]{0:T(128)}, u32[]{:S(2)}) copy-start(s32[32]{0:T(128)} %get-tuple-element.26) | copy-start | bytes 388
  31.6 1.8 %copy-start.5 = (s32[384,960]{1,0:T(8,128)S(1)}, s32[384,960]{1,0:T(8,128)}, u32[]{:S(2)}) copy-start(s32[384,960]{1,0:T(8,128)} %copy.142) | copy-start | bytes 4423684
  31.6 2.3 %copy-start.6 = (f32[384,960]{1,0:T(8,128)S(1)}, f32[384,960]{1,0:T(8,128)}, u32[]{:S(2)}) copy-start(f32[384,960]{1,0:T(8,128)} %copy.143) | copy-start | bytes 4423684
  31.6 2.3 %copy-start.15 = (s32[960]{0:T(1024)S(1)}, s32[960]{0:T(1024)}, u32[]{:S(2)}) copy-start(s32[960]{0:T(1024)} %iota.77) | copy-start | bytes 11524
  33.9 0.9 copy-start.7
  33.9 0.9 copy-start.8
  33.9 0.9 copy-start.22
  33.9 1.6 %copy-start.10 = (s32[16,96]{1,0:T(8,128)S(1)}, s32[16,96]{1,0:T(8,128)}, u32[]{:S(2)}) copy-start(s32[16,96]{1,0:T(8,128)} %copy.138) | copy-start | bytes 18436
  33.9 1.6 %copy-start.11 = (f32[16,96]{1,0:T(8,128)S(1)}, f32[16,96]{1,0:T(8,128)}, u32[]{:S(2)}) copy-start(f32[16,96]{1,0:T(8,128)} %copy.139) | copy-start | bytes 18436
  33.9 1.6 %copy-start.23 = (s32[96]{0:T(128)S(1)}, s32[96]{0:T(128)}, u32[]{:S(2)}) copy-start(s32[96]{0:T(128)} %iota.71) | copy-start | bytes 1156
  34.0 1.6 %copy-start.19 = (s32[472]{0:T(512)S(1)}, s32[472]{0:T(512)}, u32[]{:S(2)}) copy-start(s32[472]{0:T(512)} %constant.82.clone) | copy-start | bytes 5668
  34.0 1.6 %copy-start.25 = (pred[472]{0:T(512)(128)(4,1)S(1)}, pred[472]{0:T(512)(128)(4,1)}, u32[]{:S(2)}) copy-start(pred[472]{0:T(512)(128)(4,1)} %constant.83.clone) | copy-start | bytes 1420
  34.0 2.2 %copy-start.13 = (f32[10,10]{1,0:T(8,128)S(1)}, f32[10,10]{1,0:T(8,128)}, u32[]{:S(2)}) copy-start(f32[10,10]{1,0:T(8,128)} %and_convert_fusion.1) | copy-start | bytes 1204
  34.0 2.8 %copy-start.12 = (f32[10,10]{1,0:T(8,128)S(1)}, f32[10,10]{1,0:T(8,128)}, u32[]{:S(2)}) copy-start(f32[10,10]{1,0:T(8,128)} %and_convert_fusion) | copy-start | bytes 1204
  45.1 2.7 %copy-start.4 = (f32[43,12,32,12]{0,3,2,1:T(8,128)}, f32[43,12,32,12]{0,3,2,1:T(8,128)S(1)}, u32[]{:S(2)}) copy-start(f32[43,12,32,12]{0,3,2,1:T(8,128)S(1)} %pad_maximum_fusion) | copy-start | bytes 2377732
  54.8 20.0 %all-to-all-start = ((f32[32,32,128]{2,1,0:T(8,128)}), f32[32,32,128]{2,1,0:T(8,128)}, u32[]{:S(2)}, u32[]{:S(2)}) async-start(f32[32,32,128]{2,1,0:T(8,128)} %pad.21.clone), calls=%async_computation | async-start | bytes 1048576 | tf_op jit(solution)/shard_map/all_to_all | solution.py:230
  74.7 0.9 copy-start
  75.7 0.9 copy-start.2
  76.6 0.8 copy-start.3
  95.9 0.8 copy-start.1
  113.7 27.6 %all-to-all-start.2 = ((f32[16,1,3]{2,1,0:T(1,128)}), f32[16,1,3]{2,1,0:T(1,128)S(1)}, u32[]{:S(2)}, u32[]{:S(2)}) async-start(f32[16,1,3]{2,1,0:T(1,128)} %broadcast_in_dim.152), calls=%async_computation.2 | async-start | bytes 16384 | tf_op jit(solution)/shard_map/all_to_all | solution.py:331

commit v4 on v2

--- a/solution.py
+++ b/solution.py
@@ -155,7 +155,12 @@
             for d in range(4):
                 stacks[d][(k - 1) * padded[d] : k * padded[d], :] = term[offsets[d] : offsets[d] + padded[d]]
         mixed = [
-            exact_dot(mats[d][...], stacks[d][...])
+            jnp.dot(
+                mats[d][...],
+                stacks[d][...],
+                precision=lax.Precision.HIGH,
+                preferred_element_type=jnp.float32,
+            )
             for d in range(4)
         ]
         p0, p1 = padded[0], padded[1]

time: 104 us -> 99.6 us (0.958)
  Pallas kernels: 17.5 us -> 12.9 us
    pallas_call x1, Pallas kernels: 17.5 us -> 12.9 us  [local(): pl.pallas_call(functools.partial(sweeps, padded=tuple((int(v) for v in pa...]
where the time goes in v4:
time: 99.6 us; the launch traced here: 98.8 us
  starting transfers between devices  30.7 us (31%)
  local copies, waits for them, and re-layouts  21.3 us (21%)
  waiting for transfers between devices  15.2 us (15%)
  Pallas kernels  12.9 us (13%)
  blocking collectives  10.8 us (11%)
  other arithmetic  6.96 us (7%)
    all_to_all x1, starting transfers between devices, local(): all_rows = lax.all_to_all(spread, 'space', 0, 0, tiled=True)  16.8 us
    pallas_call x1, Pallas kernels, local(): pl.pallas_call(functools.partial(sweeps, padded=tuple((int(v) for v in pa...  12.9 us
    all_to_all x1, blocking collectives, local(): back = lax.all_to_all(payload, 'chaos', 0, 0, tiled=True)  10.8 us
    all_to_all x1, waiting for transfers between devices, local(): all_rows = lax.all_to_all(spread, 'space', 0, 0, tiled=True)  10.3 us
    all_to_all x1, starting transfers between devices, local(): got = lax.all_to_all(sent, 'chaos', 0, 0, tiled=True)  8.22 us
    unnamed x19, local copies, waits for them, and re-layouts  5.87 us
    all_to_all x1, waiting for transfers between devices, local(): got = lax.all_to_all(sent, 'chaos', 0, 0, tiled=True)  4.95 us
    ppermute x1, starting transfers between devices, local(): above = lax.ppermute(block[:, rows - moved:], 'space', down_pairs)  4.36 us
  transfers between devices with their start and end apart: 4, of which 2 were waited for; matrix products, arithmetic and copies ran while one was open for 13% of the time, Pallas kernels for 0%

profile of v4, /device:TPU:1, one launch (start us, length us, event | category | flops | bytes accessed | tf_op | source)
XLA Modules:
  0.0 98.8 jit_solution(9948593729573185431)
XLA Ops:
  0.6 0.7 broadcast.178
  1.3 0.7 broadcast_multiply_fusion
  2.1 0.9 pad_maximum_fusion.2
  2.9 4.4 %collective-permute-start = (f32[43,4,128]{2,1,0:T(4,128)S(1)}, f32[43,4,128]{2,1,0:T(4,128)S(1)}, u32[]{:S(2)}, u32[]{:S(2)}) collective-permute-start(f32[43,4,128]{2,1,0:T(4,128)S(1)} %pad_maximum_fusion.2), channel_id=1, source_target_pairs={{0,32},{32,64},{64,96},{96,128},{128,160},{160,192},{192,224},{224... | collective-permute-start | bytes 264200 | tf_op jit(solution)/shard_map/ppermute | solution.py:217
  7.3 1.3 %collective-permute-start.1 = (f32[43,4,128]{2,1,0:T(4,128)S(1)}, f32[43,4,128]{2,1,0:T(4,128)S(1)}, u32[]{:S(2)}, u32[]{:S(2)}) collective-permute-start(f32[43,4,128]{2,1,0:T(4,128)S(1)} %pad_maximum_fusion.2), channel_id=1, source_target_pairs={{32,0},{64,32},{96,64},{128,96},{160,128},{192,160},{224,192},{256... | collective-permute-start | bytes 264200 | tf_op jit(solution)/shard_map/ppermute | solution.py:218
  8.6 0.1 and_convert_fusion
  8.7 0.7 iota_compare_fusion
  9.4 0.7 copy.97
  10.2 0.1 reduce-window.8
  10.2 0.1 reduce.1
  10.3 0.7 fusion.5
  11.0 0.1 iota_add_fusion
  11.1 0.5 add.114
  11.6 0.6 lt.66
  12.2 0.1 and_convert_fusion.1
  12.3 0.8 select_reduce_fusion
  13.1 0.2 add_select_fusion.row_of_slot_ref
  13.2 0.7 add_select_fusion.1
  14.0 0.1 reshape.226
  14.0 0.1 reshape.227
  14.1 0.1 copy.104.slot_of_row_ref
  14.3 0.0 collective-permute-done
  14.3 0.0 collective-permute-done.1
  14.3 0.9 pad_maximum_fusion.1
  15.2 0.3 copy.114
  15.5 0.1 pad.20.clone
  15.6 0.3 fusion.4
  15.9 0.7 pad_maximum_fusion
  16.7 2.6 %slice.73 = f32[1,12,32,12]{0,3,2,1:T(8,128)} slice(f32[43,12,32,12]{0,3,2,1:T(8,128)S(1)} %pad_maximum_fusion), slice={[30:31], [0:12], [0:32], [0:12]} | slice | bytes 36864 | tf_op jit(solution)/shard_map/slice | solution.py:239
  19.3 0.2 slice_bitcast_fusion
  19.6 0.5 copy.95
  20.1 1.2 %copy.115 = f32[32,30,100]{2,1,0:T(8,128)S(1)} copy(f32[32,30,100]{1,0,2:T(8,128)S(1)} %bitcast.27) | data formatting | bytes 768000
  21.2 0.9 pad.21.clone
  22.1 8.2 %all-to-all-start = ((f32[32,32,128]{2,1,0:T(8,128)}), f32[32,32,128]{2,1,0:T(8,128)S(1)}, u32[]{:S(2)}, u32[]{:S(2)}) async-start(f32[32,32,128]{2,1,0:T(8,128)} %pad.21.clone), calls=%async_computation | async-start | bytes 1048576 | tf_op jit(solution)/shard_map/all_to_all | solution.py:235
  30.3 0.0 copy-start
  30.3 0.0 copy-start.2
  30.3 0.0 copy-start.3
  30.4 1.1 %dynamic-slice_reduce_fusion = f32[12,12]{1,0:T(8,128)S(1)} fusion(f32[1,12,32,12]{0,3,2,1:T(8,128)} %slice.73, s32[]{:T(128)S(6)} %select_n.62), kind=kLoop, calls=%fused_computation.4 | loop fusion | bytes 1156 | tf_op jit(solution)/shard_map/jit(dynamic_index_in_dim)/dynamic_slice | solution.py:239
  31.5 0.1 pad_slice_fusion.3
  31.6 4.0 %slice.72 = f32[13,10,32,10]{0,3,2,1:T(8,128)} slice(f32[43,12,32,12]{0,3,2,1:T(8,128)} %copy-done.6), slice={[30:43], [1:11], [0:32], [1:11]} | slice | bytes 332800 | tf_op jit(solution)/shard_map/slice | solution.py:237
  35.6 0.1 fusion.1
  35.7 0.1 stack_reshape.3
  35.8 0.9 constant_dynamic-slice_fusion
  36.7 0.1 copy.111
  36.8 5.0 %all-to-all-done = f32[32,32,128]{2,1,0:T(8,128)S(1)} async-done(((f32[32,32,128]{2,1,0:T(8,128)}), f32[32,32,128]{2,1,0:T(8,128)S(1)}, u32[]{:S(2)}, u32[]{:S(2)}) %all-to-all-start) | async-done | bytes 524320 | tf_op jit(solution)/shard_map/all_to_all | solution.py:235
  41.7 0.0 copy-start.1
  41.8 1.4 %copy-done.1 = f32[80,4416]{1,0:T(8,128)S(1)} copy-done((f32[80,4416]{1,0:T(8,128)S(1)}, f32[80,4416]{1,0:T(8,128)}, u32[]{:S(2)}) %copy-start.1) | copy-done | bytes 1413144
  43.1 0.7 copy-done.4
  43.8 12.9 %shard_map.122 = (f32[1024,128]{1,0:T(8,128)S(1)}, f32[8,128]{1,0:T(8,128)S(1)}) custom-call(f32[1024,128]{1,0:T(8,128)S(1)} %bitcast.24, s32[472,1]{1,0:T(8,128)S(1)} %copy.104.slot_of_row_ref, s32[1024,1]{1,0:T(8,128)S(1)} %add_select_fusion.row_of_slot_ref, f32[128,128]{1,0:T(8,128)S(1)} %copy-done.3, f32[16,128]{1,0:T(8,128)S(1)} %pad.22.field_ref, ...), custom_call_target="tpu_custom_call" | custom-call | tf_op jit(solution)/shard_map/pallas_call | solution.py:291
  56.7 0.0 copy-start.5
  56.7 0.6 copy-done.5
  57.3 0.3 copy.113
  57.6 0.1 copy.106
  57.7 0.7 slice_bitcast_fusion.1
  58.4 0.1 pad.26.clone
  58.5 10.8 %all_to_all.23 = f32[32,1,483]{2,1,0:T(1,128)S(1)} all-to-all(f32[32,1,483]{2,1,0:T(1,128)S(1)} %all_to_all.16), channel_id=1, replica_groups=mesh['space'=16,'chaos'=32] {'chaos'}, dimensions={0} | all-to-all | bytes 123648 | tf_op jit(solution)/shard_map/all_to_all | solution.py:320
  69.3 0.1 copy.107
  69.4 0.1 slice_reduce_fusion
  69.5 0.6 broadcast_in_dim.76
  70.1 16.8 %all-to-all-start.2 = ((f32[16,1,3]{2,1,0:T(1,128)}), f32[16,1,3]{2,1,0:T(1,128)S(1)}, u32[]{:S(2)}, u32[]{:S(2)}) async-start(f32[16,1,3]{2,1,0:T(1,128)} %broadcast_in_dim.76), calls=%async_computation.2 | async-start | bytes 16384 | tf_op jit(solution)/shard_map/all_to_all | solution.py:325
  87.0 0.2 copy.108
  87.2 0.7 copy.110
  88.0 10.3 %all-to-all-done.2 = f32[16,1,3]{2,1,0:T(1,128)S(1)} async-done(((f32[16,1,3]{2,1,0:T(1,128)}), f32[16,1,3]{2,1,0:T(1,128)S(1)}, u32[]{:S(2)}, u32[]{:S(2)}) %all-to-all-start.2) | async-done | bytes 224 | tf_op jit(solution)/shard_map/all_to_all | solution.py:325
  98.3 0.5 sqrt.3
  (15 shorter events, 0.2 us)
Async XLA Ops:
  2.9 11.3 %collective-permute-start = (f32[43,4,128]{2,1,0:T(4,128)S(1)}, f32[43,4,128]{2,1,0:T(4,128)S(1)}, u32[]{:S(2)}, u32[]{:S(2)}) collective-permute-start(f32[43,4,128]{2,1,0:T(4,128)S(1)} %pad_maximum_fusion.2), channel_id=1, source_target_pairs={{0,32},{32,64},{64,96},{96,128},{128,160},{160,192},{192,224},{224... | collective-permute-start | bytes 264200 | tf_op jit(solution)/shard_map/ppermute | solution.py:217
  7.3 7.0 %collective-permute-start.1 = (f32[43,4,128]{2,1,0:T(4,128)S(1)}, f32[43,4,128]{2,1,0:T(4,128)S(1)}, u32[]{:S(2)}, u32[]{:S(2)}) collective-permute-start(f32[43,4,128]{2,1,0:T(4,128)S(1)} %pad_maximum_fusion.2), channel_id=1, source_target_pairs={{32,0},{64,32},{96,64},{128,96},{160,128},{192,160},{224,192},{256... | collective-permute-start | bytes 264200 | tf_op jit(solution)/shard_map/ppermute | solution.py:218
  16.7 2.7 %copy-start.6 = (f32[43,12,32,12]{0,3,2,1:T(8,128)}, f32[43,12,32,12]{0,3,2,1:T(8,128)S(1)}, u32[]{:S(2)}) copy-start(f32[43,12,32,12]{0,3,2,1:T(8,128)S(1)} %pad_maximum_fusion) | copy-start | bytes 2377732
  22.1 19.6 %all-to-all-start = ((f32[32,32,128]{2,1,0:T(8,128)}), f32[32,32,128]{2,1,0:T(8,128)S(1)}, u32[]{:S(2)}, u32[]{:S(2)}) async-start(f32[32,32,128]{2,1,0:T(8,128)} %pad.21.clone), calls=%async_computation | async-start | bytes 1048576 | tf_op jit(solution)/shard_map/all_to_all | solution.py:235
  30.3 11.4 %copy-start = (f32[384,960]{1,0:T(8,128)S(1)}, f32[384,960]{1,0:T(8,128)}, u32[]{:S(2)}) copy-start(f32[384,960]{1,0:T(8,128)} %constant.78.clone.w2_ref) | copy-start | bytes 4423684
  30.3 11.4 %copy-start.2 = (f32[88,192]{1,0:T(8,128)S(1)}, f32[88,192]{1,0:T(8,128)}, u32[]{:S(2)}) copy-start(f32[88,192]{1,0:T(8,128)} %constant.77.clone.w1_ref) | copy-start | bytes 202756
  30.3 11.4 %copy-start.3 = (f32[128,128]{1,0:T(8,128)S(1)}, f32[128,128]{1,0:T(8,128)}, u32[]{:S(2)}) copy-start(f32[128,128]{1,0:T(8,128)} %constant.80.clone.picks_ref) | copy-start | bytes 196612
  41.7 1.4 %copy-start.1 = (f32[80,4416]{1,0:T(8,128)S(1)}, f32[80,4416]{1,0:T(8,128)}, u32[]{:S(2)}) copy-start(f32[80,4416]{1,0:T(8,128)} %constant.79.clone.w3_ref) | copy-start | bytes 4239364
  43.1 0.7 copy-start.4
  56.7 0.6 copy-start.5
  70.1 28.1 %all-to-all-start.2 = ((f32[16,1,3]{2,1,0:T(1,128)}), f32[16,1,3]{2,1,0:T(1,128)S(1)}, u32[]{:S(2)}, u32[]{:S(2)}) async-start(f32[16,1,3]{2,1,0:T(1,128)} %broadcast_in_dim.76), calls=%async_computation.2 | async-start | bytes 16384 | tf_op jit(solution)/shard_map/all_to_all | solution.py:325

commit v5 on v4

--- a/solution.py
+++ b/solution.py
@@ -121,6 +121,21 @@
     return jnp.dot(left, right, precision=lax.Precision.HIGHEST, preferred_element_type=jnp.float32)
 
 
+def pick_dot(left, right, split_left):
+    ones, values = (right, left) if split_left else (left, right)
+    ones = ones.astype(jnp.bfloat16)
+    high = values.astype(jnp.bfloat16)
+    rest = values - high.astype(jnp.float32)
+    middle = rest.astype(jnp.bfloat16)
+    low = (rest - middle.astype(jnp.float32)).astype(jnp.bfloat16)
+    total = None
+    for part in (high, middle, low):
+        pair = (part, ones) if split_left else (ones, part)
+        step = jnp.dot(*pair, preferred_element_type=jnp.float32)
+        total = step if total is None else total + step
+    return total
+
+
 def sweeps(slots_ref, slot_of_row_ref, row_of_slot_ref, picks_ref, field_ref, mask_ref,
            w0_ref, w1_ref, w2_ref, w3_ref, out_ref, part_ref,
            s0_ref, s1_ref, s2_ref, s3_ref, *, padded, offsets, cols, state_rows):
@@ -128,7 +143,7 @@
     total = slot_of_row_ref.shape[0]
     n_slots = slots_ref.shape[0]
     take = lax.broadcasted_iota(jnp.int32, (total, n_slots), 1) == slot_of_row_ref[...]
-    rhs = exact_dot(take.astype(jnp.float32), slots_ref[...])
+    rhs = pick_dot(take.astype(jnp.float32), slots_ref[...], False)
     shifts = (cols, lanes - cols, lanes - 1, 1)
 
     def near(values, shift):
@@ -188,12 +203,12 @@
             direction = rho_new * rho * direction + 2.0 * rho_new / delta * (residual / diagonal)
             direction = jnp.where(inside, direction, 0.0)
             rho = rho_new
-    own_cells = exact_dot(solution, picks_ref[...])
+    own_cells = pick_dot(solution, picks_ref[...], True)
     own_cells = jnp.concatenate(
         [own_cells, jnp.zeros((state_rows - total, own_cells.shape[1]), jnp.float32)], axis=0
     )
     put = lax.broadcasted_iota(jnp.int32, (n_slots, state_rows), 1) == row_of_slot_ref[...]
-    out_ref[...] = exact_dot(put.astype(jnp.float32), own_cells)
+    out_ref[...] = pick_dot(put.astype(jnp.float32), own_cells, False)
     part_ref[...] = partial_out
 
 

time: 99.6 us -> 96.1 us (0.965)
  Pallas kernels: 12.9 us -> 9.41 us
    pallas_call x1, Pallas kernels: 12.9 us -> 9.41 us  [local(): pl.pallas_call(functools.partial(sweeps, padded=tuple((int(v) for v in pa...]
  transfers between devices with their start and end apart: 4 -> 4, of which waited for: 2 -> 2; matrix products, arithmetic and copies ran while one was open for 13% -> 14% of each run, Pallas kernels for 0% -> 0%
where the time goes in v5:
time: 96.1 us; the launch traced here: 95.4 us
  starting transfers between devices  30.6 us (32%)
  local copies, waits for them, and re-layouts  21.4 us (22%)
  waiting for transfers between devices  15.4 us (16%)
  blocking collectives  10.8 us (11%)
  Pallas kernels  9.41 us (10%)
  other arithmetic  6.96 us (7%)
    all_to_all x1, starting transfers between devices, local(): all_rows = lax.all_to_all(spread, 'space', 0, 0, tiled=True)  16.8 us
    all_to_all x1, blocking collectives, local(): back = lax.all_to_all(payload, 'chaos', 0, 0, tiled=True)  10.8 us
    all_to_all x1, waiting for transfers between devices, local(): all_rows = lax.all_to_all(spread, 'space', 0, 0, tiled=True)  10.3 us
    pallas_call x1, Pallas kernels, local(): pl.pallas_call(functools.partial(sweeps, padded=tuple((int(v) for v in pa...  9.41 us
    all_to_all x1, starting transfers between devices, local(): got = lax.all_to_all(sent, 'chaos', 0, 0, tiled=True)  8.05 us
    unnamed x19, local copies, waits for them, and re-layouts  5.87 us
    all_to_all x1, waiting for transfers between devices, local(): got = lax.all_to_all(sent, 'chaos', 0, 0, tiled=True)  5.13 us
    ppermute x1, starting transfers between devices, local(): above = lax.ppermute(block[:, rows - moved:], 'space', down_pairs)  4.36 us
  transfers between devices with their start and end apart: 4, of which 2 were waited for; matrix products, arithmetic and copies ran while one was open for 14% of the time, Pallas kernels for 0%

profile of v5, /device:TPU:1, one launch (start us, length us, event | category | flops | bytes accessed | tf_op | source)
XLA Modules:
  0.0 95.4 jit_solution(12606289765868192464)
XLA Ops:
  0.6 0.7 broadcast.178
  1.3 0.7 broadcast_multiply_fusion
  2.1 0.9 pad_maximum_fusion.2
  2.9 4.4 %collective-permute-start = (f32[43,4,128]{2,1,0:T(4,128)S(1)}, f32[43,4,128]{2,1,0:T(4,128)S(1)}, u32[]{:S(2)}, u32[]{:S(2)}) collective-permute-start(f32[43,4,128]{2,1,0:T(4,128)S(1)} %pad_maximum_fusion.2), channel_id=1, source_target_pairs={{0,32},{32,64},{64,96},{96,128},{128,160},{160,192},{192,224},{224... | collective-permute-start | bytes 264200 | tf_op jit(solution)/shard_map/ppermute | solution.py:232
  7.3 1.3 %collective-permute-start.1 = (f32[43,4,128]{2,1,0:T(4,128)S(1)}, f32[43,4,128]{2,1,0:T(4,128)S(1)}, u32[]{:S(2)}, u32[]{:S(2)}) collective-permute-start(f32[43,4,128]{2,1,0:T(4,128)S(1)} %pad_maximum_fusion.2), channel_id=1, source_target_pairs={{32,0},{64,32},{96,64},{128,96},{160,128},{192,160},{224,192},{256... | collective-permute-start | bytes 264200 | tf_op jit(solution)/shard_map/ppermute | solution.py:233
  8.6 0.1 and_convert_fusion
  8.7 0.7 iota_compare_fusion
  9.4 0.7 copy.97
  10.2 0.1 reduce-window.8
  10.2 0.1 reduce.1
  10.3 0.7 fusion.5
  11.0 0.1 iota_add_fusion
  11.1 0.5 add.114
  11.6 0.6 lt.66
  12.2 0.1 and_convert_fusion.1
  12.3 0.8 select_reduce_fusion
  13.1 0.2 add_select_fusion.row_of_slot_ref
  13.2 0.7 add_select_fusion.1
  14.0 0.1 reshape.226
  14.0 0.1 reshape.227
  14.1 0.1 copy.104.slot_of_row_ref
  14.3 0.0 collective-permute-done
  14.3 0.0 collective-permute-done.1
  14.3 0.9 pad_maximum_fusion.1
  15.2 0.3 copy.114
  15.5 0.1 pad.20.clone
  15.6 0.3 fusion.4
  15.9 0.7 pad_maximum_fusion
  16.7 2.6 %slice.73 = f32[1,12,32,12]{0,3,2,1:T(8,128)} slice(f32[43,12,32,12]{0,3,2,1:T(8,128)S(1)} %pad_maximum_fusion), slice={[30:31], [0:12], [0:32], [0:12]} | slice | bytes 36864 | tf_op jit(solution)/shard_map/slice | solution.py:254
  19.3 0.2 slice_bitcast_fusion
  19.6 0.5 copy.95
  20.1 1.2 %copy.115 = f32[32,30,100]{2,1,0:T(8,128)S(1)} copy(f32[32,30,100]{1,0,2:T(8,128)S(1)} %bitcast.27) | data formatting | bytes 768000
  21.2 0.9 pad.21.clone
  22.1 8.0 %all-to-all-start = ((f32[32,32,128]{2,1,0:T(8,128)}), f32[32,32,128]{2,1,0:T(8,128)S(1)}, u32[]{:S(2)}, u32[]{:S(2)}) async-start(f32[32,32,128]{2,1,0:T(8,128)} %pad.21.clone), calls=%async_computation | async-start | bytes 1048576 | tf_op jit(solution)/shard_map/all_to_all | solution.py:250
  30.1 0.0 copy-start
  30.2 0.0 copy-start.2
  30.2 0.0 copy-start.3
  30.2 1.1 %dynamic-slice_reduce_fusion = f32[12,12]{1,0:T(8,128)S(1)} fusion(f32[1,12,32,12]{0,3,2,1:T(8,128)} %slice.73, s32[]{:T(128)S(6)} %select_n.62), kind=kLoop, calls=%fused_computation.4 | loop fusion | bytes 1156 | tf_op jit(solution)/shard_map/jit(dynamic_index_in_dim)/dynamic_slice | solution.py:254
  31.3 0.1 pad_slice_fusion.3
  31.4 4.0 %slice.72 = f32[13,10,32,10]{0,3,2,1:T(8,128)} slice(f32[43,12,32,12]{0,3,2,1:T(8,128)} %copy-done.6), slice={[30:43], [1:11], [0:32], [1:11]} | slice | bytes 332800 | tf_op jit(solution)/shard_map/slice | solution.py:252
  35.4 0.1 fusion.1
  35.5 0.1 stack_reshape.3
  35.6 0.9 constant_dynamic-slice_fusion
  36.5 0.1 copy.111
  36.6 5.1 %all-to-all-done = f32[32,32,128]{2,1,0:T(8,128)S(1)} async-done(((f32[32,32,128]{2,1,0:T(8,128)}), f32[32,32,128]{2,1,0:T(8,128)S(1)}, u32[]{:S(2)}, u32[]{:S(2)}) %all-to-all-start) | async-done | bytes 524320 | tf_op jit(solution)/shard_map/all_to_all | solution.py:250
  41.7 0.0 copy-start.1
  41.8 1.4 %copy-done.1 = f32[80,4416]{1,0:T(8,128)S(1)} copy-done((f32[80,4416]{1,0:T(8,128)S(1)}, f32[80,4416]{1,0:T(8,128)}, u32[]{:S(2)}) %copy-start.1) | copy-done | bytes 1413144
  43.1 0.7 copy-done.4
  43.8 9.4 %shard_map.122 = (f32[1024,128]{1,0:T(8,128)S(1)}, f32[8,128]{1,0:T(8,128)S(1)}) custom-call(f32[1024,128]{1,0:T(8,128)S(1)} %bitcast.24, s32[472,1]{1,0:T(8,128)S(1)} %copy.104.slot_of_row_ref, s32[1024,1]{1,0:T(8,128)S(1)} %add_select_fusion.row_of_slot_ref, f32[128,128]{1,0:T(8,128)S(1)} %copy-done.3, f32[16,128]{1,0:T(8,128)S(1)} %pad.22.field_ref, ...), custom_call_target="tpu_custom_call" | custom-call | tf_op jit(solution)/shard_map/pallas_call | solution.py:306
  53.2 0.0 copy-start.5
  53.2 0.6 copy-done.5
  53.8 0.3 copy.113
  54.1 0.1 copy.106
  54.2 0.7 slice_bitcast_fusion.1
  54.9 0.1 pad.26.clone
  55.1 10.8 %all_to_all.23 = f32[32,1,483]{2,1,0:T(1,128)S(1)} all-to-all(f32[32,1,483]{2,1,0:T(1,128)S(1)} %all_to_all.16), channel_id=1, replica_groups=mesh['space'=16,'chaos'=32] {'chaos'}, dimensions={0} | all-to-all | bytes 123648 | tf_op jit(solution)/shard_map/all_to_all | solution.py:335
  65.8 0.1 copy.107
  66.0 0.1 slice_reduce_fusion
  66.1 0.6 broadcast_in_dim.76
  66.7 16.8 %all-to-all-start.2 = ((f32[16,1,3]{2,1,0:T(1,128)}), f32[16,1,3]{2,1,0:T(1,128)S(1)}, u32[]{:S(2)}, u32[]{:S(2)}) async-start(f32[16,1,3]{2,1,0:T(1,128)} %broadcast_in_dim.76), calls=%async_computation.2 | async-start | bytes 16384 | tf_op jit(solution)/shard_map/all_to_all | solution.py:340
  83.6 0.2 copy.108
  83.8 0.7 copy.110
  84.5 10.3 %all-to-all-done.2 = f32[16,1,3]{2,1,0:T(1,128)S(1)} async-done(((f32[16,1,3]{2,1,0:T(1,128)}), f32[16,1,3]{2,1,0:T(1,128)S(1)}, u32[]{:S(2)}, u32[]{:S(2)}) %all-to-all-start.2) | async-done | bytes 224 | tf_op jit(solution)/shard_map/all_to_all | solution.py:340
  94.8 0.5 sqrt.3
  (15 shorter events, 0.2 us)
Async XLA Ops:
  2.9 11.3 %collective-permute-start = (f32[43,4,128]{2,1,0:T(4,128)S(1)}, f32[43,4,128]{2,1,0:T(4,128)S(1)}, u32[]{:S(2)}, u32[]{:S(2)}) collective-permute-start(f32[43,4,128]{2,1,0:T(4,128)S(1)} %pad_maximum_fusion.2), channel_id=1, source_target_pairs={{0,32},{32,64},{64,96},{96,128},{128,160},{160,192},{192,224},{224... | collective-permute-start | bytes 264200 | tf_op jit(solution)/shard_map/ppermute | solution.py:232
  7.3 7.0 %collective-permute-start.1 = (f32[43,4,128]{2,1,0:T(4,128)S(1)}, f32[43,4,128]{2,1,0:T(4,128)S(1)}, u32[]{:S(2)}, u32[]{:S(2)}) collective-permute-start(f32[43,4,128]{2,1,0:T(4,128)S(1)} %pad_maximum_fusion.2), channel_id=1, source_target_pairs={{32,0},{64,32},{96,64},{128,96},{160,128},{192,160},{224,192},{256... | collective-permute-start | bytes 264200 | tf_op jit(solution)/shard_map/ppermute | solution.py:233
  16.7 2.7 %copy-start.6 = (f32[43,12,32,12]{0,3,2,1:T(8,128)}, f32[43,12,32,12]{0,3,2,1:T(8,128)S(1)}, u32[]{:S(2)}) copy-start(f32[43,12,32,12]{0,3,2,1:T(8,128)S(1)} %pad_maximum_fusion) | copy-start | bytes 2377732
  22.1 19.6 %all-to-all-start = ((f32[32,32,128]{2,1,0:T(8,128)}), f32[32,32,128]{2,1,0:T(8,128)S(1)}, u32[]{:S(2)}, u32[]{:S(2)}) async-start(f32[32,32,128]{2,1,0:T(8,128)} %pad.21.clone), calls=%async_computation | async-start | bytes 1048576 | tf_op jit(solution)/shard_map/all_to_all | solution.py:250
  30.1 11.6 %copy-start = (f32[384,960]{1,0:T(8,128)S(1)}, f32[384,960]{1,0:T(8,128)}, u32[]{:S(2)}) copy-start(f32[384,960]{1,0:T(8,128)} %constant.78.clone.w2_ref) | copy-start | bytes 4423684
  30.2 11.6 %copy-start.2 = (f32[88,192]{1,0:T(8,128)S(1)}, f32[88,192]{1,0:T(8,128)}, u32[]{:S(2)}) copy-start(f32[88,192]{1,0:T(8,128)} %constant.77.clone.w1_ref) | copy-start | bytes 202756
  30.2 11.6 %copy-start.3 = (f32[128,128]{1,0:T(8,128)S(1)}, f32[128,128]{1,0:T(8,128)}, u32[]{:S(2)}) copy-start(f32[128,128]{1,0:T(8,128)} %constant.80.clone.picks_ref) | copy-start | bytes 196612
  41.7 1.4 %copy-start.1 = (f32[80,4416]{1,0:T(8,128)S(1)}, f32[80,4416]{1,0:T(8,128)}, u32[]{:S(2)}) copy-start(f32[80,4416]{1,0:T(8,128)} %constant.79.clone.w3_ref) | copy-start | bytes 4239364
  43.1 0.7 copy-start.4
  53.2 0.6 copy-start.5
  66.7 28.1 %all-to-all-start.2 = ((f32[16,1,3]{2,1,0:T(1,128)}), f32[16,1,3]{2,1,0:T(1,128)S(1)}, u32[]{:S(2)}, u32[]{:S(2)}) async-start(f32[16,1,3]{2,1,0:T(1,128)} %broadcast_in_dim.76), calls=%async_computation.2 | async-start | bytes 16384 | tf_op jit(solution)/shard_map/all_to_all | solution.py:340

commit v6 on v5

--- a/solution.py
+++ b/solution.py
@@ -329,13 +329,14 @@
         [
             by_slot_out.reshape(n_chaos, chunk),
             jnp.broadcast_to(partials[None, :], (n_chaos, ITERS)),
+            jnp.zeros((n_chaos, -(-(chunk + ITERS) // 128) * 128 - chunk - ITERS), jnp.float32),
         ],
         axis=1,
     )
     back = lax.all_to_all(payload, "chaos", 0, 0, tiled=True)
     out = back[:, :chunk].reshape(n_chaos, cap, rows, width)
     out = jnp.transpose(out, (1, 2, 0, 3)).reshape(cap, rows, cols)
-    row_sum = jnp.sum(back[:, chunk:], axis=0)
+    row_sum = jnp.sum(back[:, chunk : chunk + ITERS], axis=0)
     spread = jnp.broadcast_to(row_sum[None, :], (n_space, ITERS))
     all_rows = lax.all_to_all(spread, "space", 0, 0, tiled=True)
     norms = jnp.sqrt(jnp.sum(all_rows, axis=0))

time: 96.1 us -> 97.5 us (1.015)
  no operation moved by 1% of the time
where the time goes in v6:
time: 97.5 us; the launch traced here: 96.7 us
  starting transfers between devices  30.6 us (31%)
  local copies, waits for them, and re-layouts  22 us (23%)
  waiting for transfers between devices  15.4 us (16%)
  blocking collectives  10.8 us (11%)
  Pallas kernels  9.41 us (10%)
  other arithmetic  7.63 us (8%)
    all_to_all x1, starting transfers between devices, local(): all_rows = lax.all_to_all(spread, 'space', 0, 0, tiled=True)  16.8 us
    all_to_all x1, blocking collectives, local(): back = lax.all_to_all(payload, 'chaos', 0, 0, tiled=True)  10.8 us
    all_to_all x1, waiting for transfers between devices, local(): all_rows = lax.all_to_all(spread, 'space', 0, 0, tiled=True)  10.3 us
    pallas_call x1, Pallas kernels, local(): pl.pallas_call(functools.partial(sweeps, padded=tuple((int(v) for v in pa...  9.41 us
    all_to_all x1, starting transfers between devices, local(): got = lax.all_to_all(sent, 'chaos', 0, 0, tiled=True)  8.05 us
    unnamed x19, local copies, waits for them, and re-layouts  5.87 us
    all_to_all x1, waiting for transfers between devices, local(): got = lax.all_to_all(sent, 'chaos', 0, 0, tiled=True)  5.13 us
    ppermute x1, starting transfers between devices, local(): above = lax.ppermute(block[:, rows - moved:], 'space', down_pairs)  4.36 us
  transfers between devices with their start and end apart: 4, of which 2 were waited for; matrix products, arithmetic and copies ran while one was open for 14% of the time, Pallas kernels for 0%

profile of v6, /device:TPU:1, one launch (start us, length us, event | category | flops | bytes accessed | tf_op | source)
XLA Modules:
  0.0 96.7 jit_solution(11732815419331401928)
XLA Ops:
  0.6 0.7 broadcast.180
  1.3 0.7 broadcast_multiply_fusion
  2.1 0.9 pad_maximum_fusion.2
  2.9 4.4 %collective-permute-start = (f32[43,4,128]{2,1,0:T(4,128)S(1)}, f32[43,4,128]{2,1,0:T(4,128)S(1)}, u32[]{:S(2)}, u32[]{:S(2)}) collective-permute-start(f32[43,4,128]{2,1,0:T(4,128)S(1)} %pad_maximum_fusion.2), channel_id=1, source_target_pairs={{0,32},{32,64},{64,96},{96,128},{128,160},{160,192},{192,224},{224... | collective-permute-start | bytes 264200 | tf_op jit(solution)/shard_map/ppermute | solution.py:232
  7.3 1.3 %collective-permute-start.1 = (f32[43,4,128]{2,1,0:T(4,128)S(1)}, f32[43,4,128]{2,1,0:T(4,128)S(1)}, u32[]{:S(2)}, u32[]{:S(2)}) collective-permute-start(f32[43,4,128]{2,1,0:T(4,128)S(1)} %pad_maximum_fusion.2), channel_id=1, source_target_pairs={{32,0},{64,32},{96,64},{128,96},{160,128},{192,160},{224,192},{256... | collective-permute-start | bytes 264200 | tf_op jit(solution)/shard_map/ppermute | solution.py:233
  8.6 0.1 and_convert_fusion
  8.7 0.7 iota_compare_fusion
  9.4 0.7 copy.97
  10.2 0.1 reduce-window.8
  10.2 0.1 reduce.1
  10.3 0.7 fusion.5
  11.0 0.1 iota_add_fusion
  11.1 0.5 add.114
  11.6 0.6 lt.66
  12.2 0.1 and_convert_fusion.1
  12.3 0.8 select_reduce_fusion
  13.1 0.2 add_select_fusion.row_of_slot_ref
  13.2 0.7 add_select_fusion.1
  14.0 0.1 reshape.226
  14.0 0.1 reshape.227
  14.1 0.1 copy.104.slot_of_row_ref
  14.3 0.7 pad.27.clone
  14.9 0.9 pad_maximum_fusion.1
  15.9 0.3 copy.114
  16.2 0.1 pad.20.clone
  16.3 0.3 fusion.4
  16.6 0.7 pad_maximum_fusion
  17.3 2.6 %slice.73 = f32[1,12,32,12]{0,3,2,1:T(8,128)} slice(f32[43,12,32,12]{0,3,2,1:T(8,128)S(1)} %pad_maximum_fusion), slice={[30:31], [0:12], [0:32], [0:12]} | slice | bytes 36864 | tf_op jit(solution)/shard_map/slice | solution.py:254
  20.0 0.2 slice_bitcast_fusion
  20.2 0.5 copy.95
  20.7 1.2 %copy.115 = f32[32,30,100]{2,1,0:T(8,128)S(1)} copy(f32[32,30,100]{1,0,2:T(8,128)S(1)} %bitcast.27) | data formatting | bytes 768000
  21.9 0.9 pad.21.clone
  22.7 8.0 %all-to-all-start = ((f32[32,32,128]{2,1,0:T(8,128)}), f32[32,32,128]{2,1,0:T(8,128)S(1)}, u32[]{:S(2)}, u32[]{:S(2)}) async-start(f32[32,32,128]{2,1,0:T(8,128)} %pad.21.clone), calls=%async_computation | async-start | bytes 1048576 | tf_op jit(solution)/shard_map/all_to_all | solution.py:250
  30.8 0.0 copy-start
  30.8 0.0 copy-start.2
  30.8 0.0 copy-start.3
  30.8 1.1 %dynamic-slice_reduce_fusion = f32[12,12]{1,0:T(8,128)S(1)} fusion(f32[1,12,32,12]{0,3,2,1:T(8,128)} %slice.73, s32[]{:T(128)S(6)} %select_n.62), kind=kLoop, calls=%fused_computation.4 | loop fusion | bytes 1156 | tf_op jit(solution)/shard_map/jit(dynamic_index_in_dim)/dynamic_slice | solution.py:254
  32.0 0.1 pad_slice_fusion.3
  32.0 4.0 %slice.72 = f32[13,10,32,10]{0,3,2,1:T(8,128)} slice(f32[43,12,32,12]{0,3,2,1:T(8,128)} %copy-done.6), slice={[30:43], [1:11], [0:32], [1:11]} | slice | bytes 332800 | tf_op jit(solution)/shard_map/slice | solution.py:252
  36.1 0.1 fusion.1
  36.2 0.1 stack_reshape.3
  36.2 0.9 constant_dynamic-slice_fusion
  37.2 0.1 copy.111
  37.3 5.1 %all-to-all-done = f32[32,32,128]{2,1,0:T(8,128)S(1)} async-done(((f32[32,32,128]{2,1,0:T(8,128)}), f32[32,32,128]{2,1,0:T(8,128)S(1)}, u32[]{:S(2)}, u32[]{:S(2)}) %all-to-all-start) | async-done | bytes 524320 | tf_op jit(solution)/shard_map/all_to_all | solution.py:250
  42.4 0.0 copy-start.1
  42.4 1.4 %copy-done.1 = f32[80,4416]{1,0:T(8,128)S(1)} copy-done((f32[80,4416]{1,0:T(8,128)S(1)}, f32[80,4416]{1,0:T(8,128)}, u32[]{:S(2)}) %copy-start.1) | copy-done | bytes 1413144
  43.8 0.7 copy-done.4
  44.5 9.4 %shard_map.122 = (f32[1024,128]{1,0:T(8,128)S(1)}, f32[8,128]{1,0:T(8,128)S(1)}) custom-call(f32[1024,128]{1,0:T(8,128)S(1)} %bitcast.24, s32[472,1]{1,0:T(8,128)S(1)} %copy.104.slot_of_row_ref, s32[1024,1]{1,0:T(8,128)S(1)} %add_select_fusion.row_of_slot_ref, f32[128,128]{1,0:T(8,128)S(1)} %copy-done.3, f32[16,128]{1,0:T(8,128)S(1)} %pad.22.field_ref, ...), custom_call_target="tpu_custom_call" | custom-call | tf_op jit(solution)/shard_map/pallas_call | solution.py:306
  53.9 0.0 copy-start.5
  53.9 0.6 copy-done.5
  54.5 0.3 copy.113
  54.8 0.1 copy.106
  54.9 0.7 slice_bitcast_fusion.1
  55.6 0.1 pad.26.clone
  55.7 0.7 maximum_maximum_fusion
  56.4 10.8 %all_to_all.23 = f32[32,1,512]{2,1,0:T(1,128)S(1)} all-to-all(f32[32,1,512]{2,1,0:T(1,128)S(1)} %all_to_all.16), channel_id=1, replica_groups=mesh['space'=16,'chaos'=32] {'chaos'}, dimensions={0} | all-to-all | bytes 131072 | tf_op jit(solution)/shard_map/all_to_all | solution.py:336
  67.2 0.1 copy.107
  67.3 0.1 slice_reduce_fusion
  67.4 0.6 broadcast_in_dim.80
  68.0 16.8 %all-to-all-start.2 = ((f32[16,1,3]{2,1,0:T(1,128)}), f32[16,1,3]{2,1,0:T(1,128)S(1)}, u32[]{:S(2)}, u32[]{:S(2)}) async-start(f32[16,1,3]{2,1,0:T(1,128)} %broadcast_in_dim.80), calls=%async_computation.2 | async-start | bytes 16384 | tf_op jit(solution)/shard_map/all_to_all | solution.py:341
  84.9 0.2 copy.108
  85.1 0.7 copy.110
  85.9 10.3 %all-to-all-done.2 = f32[16,1,3]{2,1,0:T(1,128)S(1)} async-done(((f32[16,1,3]{2,1,0:T(1,128)}), f32[16,1,3]{2,1,0:T(1,128)S(1)}, u32[]{:S(2)}, u32[]{:S(2)}) %all-to-all-start.2) | async-done | bytes 224 | tf_op jit(solution)/shard_map/all_to_all | solution.py:341
  96.2 0.5 sqrt.3
  (17 shorter events, 0.2 us)
Async XLA Ops:
  2.9 12.0 %collective-permute-start = (f32[43,4,128]{2,1,0:T(4,128)S(1)}, f32[43,4,128]{2,1,0:T(4,128)S(1)}, u32[]{:S(2)}, u32[]{:S(2)}) collective-permute-start(f32[43,4,128]{2,1,0:T(4,128)S(1)} %pad_maximum_fusion.2), channel_id=1, source_target_pairs={{0,32},{32,64},{64,96},{96,128},{128,160},{160,192},{192,224},{224... | collective-permute-start | bytes 264200 | tf_op jit(solution)/shard_map/ppermute | solution.py:232
  7.3 7.6 %collective-permute-start.1 = (f32[43,4,128]{2,1,0:T(4,128)S(1)}, f32[43,4,128]{2,1,0:T(4,128)S(1)}, u32[]{:S(2)}, u32[]{:S(2)}) collective-permute-start(f32[43,4,128]{2,1,0:T(4,128)S(1)} %pad_maximum_fusion.2), channel_id=1, source_target_pairs={{32,0},{64,32},{96,64},{128,96},{160,128},{192,160},{224,192},{256... | collective-permute-start | bytes 264200 | tf_op jit(solution)/shard_map/ppermute | solution.py:233
  17.3 2.7 %copy-start.6 = (f32[43,12,32,12]{0,3,2,1:T(8,128)}, f32[43,12,32,12]{0,3,2,1:T(8,128)S(1)}, u32[]{:S(2)}) copy-start(f32[43,12,32,12]{0,3,2,1:T(8,128)S(1)} %pad_maximum_fusion) | copy-start | bytes 2377732
  22.7 19.6 %all-to-all-start = ((f32[32,32,128]{2,1,0:T(8,128)}), f32[32,32,128]{2,1,0:T(8,128)S(1)}, u32[]{:S(2)}, u32[]{:S(2)}) async-start(f32[32,32,128]{2,1,0:T(8,128)} %pad.21.clone), calls=%async_computation | async-start | bytes 1048576 | tf_op jit(solution)/shard_map/all_to_all | solution.py:250
  30.8 11.6 %copy-start = (f32[384,960]{1,0:T(8,128)S(1)}, f32[384,960]{1,0:T(8,128)}, u32[]{:S(2)}) copy-start(f32[384,960]{1,0:T(8,128)} %constant.79.clone.w2_ref) | copy-start | bytes 4423684
  30.8 11.6 %copy-start.2 = (f32[88,192]{1,0:T(8,128)S(1)}, f32[88,192]{1,0:T(8,128)}, u32[]{:S(2)}) copy-start(f32[88,192]{1,0:T(8,128)} %constant.78.clone.w1_ref) | copy-start | bytes 202756
  30.8 11.6 %copy-start.3 = (f32[128,128]{1,0:T(8,128)S(1)}, f32[128,128]{1,0:T(8,128)}, u32[]{:S(2)}) copy-start(f32[128,128]{1,0:T(8,128)} %constant.81.clone.picks_ref) | copy-start | bytes 196612
  42.4 1.4 %copy-start.1 = (f32[80,4416]{1,0:T(8,128)S(1)}, f32[80,4416]{1,0:T(8,128)}, u32[]{:S(2)}) copy-start(f32[80,4416]{1,0:T(8,128)} %constant.80.clone.w3_ref) | copy-start | bytes 4239364
  43.8 0.7 copy-start.4
  53.9 0.6 copy-start.5
  68.0 28.1 %all-to-all-start.2 = ((f32[16,1,3]{2,1,0:T(1,128)}), f32[16,1,3]{2,1,0:T(1,128)S(1)}, u32[]{:S(2)}, u32[]{:S(2)}) async-start(f32[16,1,3]{2,1,0:T(1,128)} %broadcast_in_dim.80), calls=%async_computation.2 | async-start | bytes 16384 | tf_op jit(solution)/shard_map/all_to_all | solution.py:341
